TPU v7x, 128 devices: a whole 4x4x4 slice. The times are simulated.
128 devices in a mesh: elem: 16 (over x, z), sub: 8 (over y, core).
Axes of the slice: x: 4, y: 4, z: 4, core: 2. Of those that a mesh axis runs over, the one named last changes fastest.
Arguments:
- load_vector: float32 [125, 147456], P(None, ('elem', 'sub')), may hold values from -6 to 6
- fine_scale: float32 [147456], P(('elem', 'sub')), may hold values from 0.3 to 3
- coarse_scale: float32 [32768], P(('elem', 'sub')), may hold values from 0.3 to 3
- parent_owner: int32 [147456], P(('elem', 'sub')), may hold values from 0 to 127, as said below
- parent_pos: int32 [147456], P(('elem', 'sub')), may hold values from 0 to 17, as said below
- child_code: int32 [147456], P(('elem', 'sub')), may hold values from 0 to 8, as said below
- arrival_slot: int32 [294912], P(('elem', 'sub')), may hold values from 0 to 256, as said below
- fine_local: int32 [884736], P(('elem', 'sub')), may hold values from -1 to 6911, as said below
- fine_left: int32 [36864], P(('elem', 'sub')), may hold values from 0 to 6911, as said below
- fine_right: int32 [36864], P(('elem', 'sub')), may hold values from 0 to 6911, as said below
- coarse_local: int32 [196608], P(('elem', 'sub')), may hold values from -1 to 1535, as said below
- coarse_left: int32 [8192], P(('elem', 'sub')), may hold values from 0 to 1535, as said below
- coarse_right: int32 [8192], P(('elem', 'sub')), may hold values from 0 to 1535, as said below
Outputs:
- solution: float32 [125, 147456], P(None, ('elem', 'sub'))
- residual: float32 [125, 147456], P(None, ('elem', 'sub'))
Inputs may be any that keep to these rules, and one draw needn't show every extreme that they name: `parent_owner`: each device sends at most 18 fine elements to one owner; some pair of devices reaches 18. `parent_pos`: the fine elements that one device sends to one owner hold distinct slots 0, 1, and so on. `child_code`: 0 to 7: the octant of a refined parent that the element fills; 8: the element equals its unrefined parent. Every coarse element has eight children with codes 0 to 7 or one with code 8. `arrival_slot`: entry j * 18 + k on device o is the local coarse element that receives slot k of device j's message, or 256 where device j sends fewer than k + 1 elements to o; it matches the fine element of device j with parent_owner o and parent_pos k. `fine_local`: local face ids; the pairing is symmetric; faces in the left or right list or on the boundary have -1. `fine_left`: local face ids, distinct, disjoint from the right list; entry k on a device meets entry k of fine_right on the previous device. `fine_right`: local face ids, distinct; entry k on a device meets entry k of fine_left on the next device. `coarse_local`: local face ids; the pairing is symmetric; faces in the left or right list or on the boundary have -1. `coarse_left`: local face ids, distinct, disjoint from the right list; entry k on a device meets entry k of coarse_right on the previous device. `coarse_right`: local face ids, distinct; entry k on a device meets entry k of coarse_left on the next device.
All inputs are finite; a program needn't handle non-finite values.
Results may differ from a plain program's by a relative error of at most 0.0003.
Values sent between devices are 32-bit elements; how exact they have to be, the bound alone decides.
No kernel may reach another device: no remote copies, remote signals or barrier semaphores. Data moves between devices by JAX's collectives and lax.ppermute only.
A program may use at most 64 MiB of HBM per device.

v0:
```python
import math

import jax
import jax.numpy as jnp
import numpy as np
from jax import lax
from jax.sharding import PartitionSpec as P

highest = lax.Precision.HIGHEST
penalty_weight = 20.0
lower_share = 0.125
AXES = ("elem", "sub")


def passed_along(block, axis, distance):
    devices = range(lax.axis_size(axis))
    route = [(i - distance, i) for i in devices if i - distance in devices]
    return lax.ppermute(block, axis, route)


def lagrange_rows(points, gll_points):
    values = np.ones((points.shape[0], 5))
    for column in range(5):
        for other_node in range(5):
            if other_node != column:
                values[:, column] *= (points - gll_points[other_node]) / (
                    gll_points[column] - gll_points[other_node]
                )
    return values


def element_tables():
    root_value = math.sqrt(3.0 / 7.0)
    gll_points = np.array([-1.0, -root_value, 0.0, root_value, 1.0])
    gll_weights = np.array([0.1, 49.0 / 90.0, 32.0 / 45.0, 49.0 / 90.0, 0.1])
    identity_mask = np.arange(5)[:, None] == np.arange(5)[None, :]
    spread = gll_points[:, None] - gll_points[None, :]
    spread = np.where(identity_mask, 1.0, spread)
    factor = np.prod(spread, axis=1)
    derive = factor[:, None] / factor[None, :] / spread
    diag_values = np.sum(1.0 / spread, axis=1) - 1.0
    derive = np.where(identity_mask, diag_values[:, None], derive)
    stiff_line = derive.T @ (gll_weights[:, None] * derive)
    mass_line = np.where(identity_mask, gll_weights[None, :], 0.0)
    stiffness = (
        np.kron(np.kron(stiff_line, mass_line), mass_line)
        + np.kron(np.kron(mass_line, stiff_line), mass_line)
        + np.kron(np.kron(mass_line, mass_line), stiff_line)
    )
    extract = np.zeros((150, 125))
    face_weight = np.zeros((6, 25))
    face_nodes = np.zeros((6, 25), np.int64)
    for normal in range(3):
        for side_pick in range(2):
            face_id = 2 * normal + side_pick
            for first_pos in range(5):
                for second_pos in range(5):
                    triple = [first_pos, second_pos]
                    triple.insert(normal, 4 * side_pick)
                    node_id = 25 * triple[0] + 5 * triple[1] + triple[2]
                    extract[25 * face_id + 5 * first_pos + second_pos, node_id] = 1.0
                    face_nodes[face_id, 5 * first_pos + second_pos] = node_id
                    face_weight[face_id, 5 * first_pos + second_pos] = (
                        gll_weights[first_pos] * gll_weights[second_pos]
                    )
    face_diag = extract.T @ face_weight.reshape(150)
    node_range = np.arange(125)
    stiff_diag = stiffness[node_range, node_range].copy()
    upper_bound = max(2.0, float(np.max(np.sum(np.abs(stiffness), axis=1) / stiff_diag)))
    halves = np.stack(
        [
            lagrange_rows((gll_points - 1.0) / 2.0, gll_points),
            lagrange_rows((gll_points + 1.0) / 2.0, gll_points),
        ]
    )
    return (stiffness, extract, face_weight, face_diag, stiff_diag, upper_bound, halves, face_nodes)


def to_bf16_grid(values):
    return lax.reduce_precision(values, exponent_bits=8, mantissa_bits=7)


def split3(values):
    high = to_bf16_grid(values)
    rest = values - high
    middle = to_bf16_grid(rest)
    low = rest - middle
    return tuple(part.astype(jnp.bfloat16) for part in (high, middle, low))


def place(onehot, values):
    rows, lanes = values.shape
    width = -(-lanes // 128) * 128
    parts = [jnp.pad(part, ((0, 0), (0, width - lanes))) for part in split3(values)]
    out = jnp.dot(onehot, jnp.concatenate(parts, axis=1), preferred_element_type=jnp.float32)
    total = (out[:, :width] + out[:, width : 2 * width]) + out[:, 2 * width :]
    return total[:, :lanes]


def chebyshev(start, residual_now, operator_fn, inverse_diag, upper_bound, keep_last):
    low_end = upper_bound * lower_share
    center = 0.5 * (upper_bound + low_end)
    radius = 0.5 * (upper_bound - low_end)
    sigma_value = center / radius
    rho_value = 1.0 / sigma_value
    solution = start
    update = inverse_diag * residual_now / center
    for turn_index in range(3):
        solution = solution + update
        if turn_index < 2 or keep_last:
            residual_now = residual_now - operator_fn(update)
        if turn_index < 2:
            rho_next = 1.0 / (2.0 * sigma_value - rho_value)
            update = (
                rho_next * rho_value * update
                + 2.0 * rho_next / radius * inverse_diag * residual_now
            )
            rho_value = rho_next
    return (solution, residual_now)


def onehot_of(rows_ids, column_ids):
    return (rows_ids[:, None] == column_ids[None, :]).astype(jnp.bfloat16)


def level_plan(local_ids, left_ids, right_ids):
    face_count = local_ids.shape[0]
    has_local = local_ids >= 0
    source = jnp.where(has_local, local_ids, 0)
    send_ids = jnp.concatenate([left_ids, right_ids])
    onehot = onehot_of(jnp.arange(face_count, dtype=jnp.int32), send_ids)
    return has_local, source, send_ids, onehot


def apply_level(vector_t, scale_col, plan, mats):
    has_local, source, send_ids, onehot = plan
    stiffness_t, pick, fold, weight = mats
    elem_count = vector_t.shape[0]
    shared = send_ids.shape[0] // 2
    faces = jnp.concatenate(
        [jnp.dot(vector_t, pick[f], precision=highest) for f in range(6)], axis=0
    )
    sent = faces[send_ids]
    from_left = passed_along(sent[shared:], AXES, 1)
    from_right = passed_along(sent[:shared], AXES, -1)
    partner = jnp.where(has_local[:, None], faces[source], 0.0)
    received = jnp.concatenate([from_left, from_right], axis=0)
    partner = partner + place(onehot, received)
    jump = (faces - partner).reshape(6, elem_count, 128) * weight[:, None, :]
    folded = lax.dot_general(
        jump, fold, (((2,), (1,)), ((0,), (0,))), precision=highest
    ).sum(axis=0)
    interior = scale_col * jnp.dot(vector_t, stiffness_t, precision=highest)
    return interior + folded


def interpolate_t(values_t, code_row, mats):
    mixed = jnp.dot(values_t, mats, precision=highest)
    out = jnp.zeros_like(values_t)
    for q in range(9):
        out = jnp.where(code_row[:, None] == q, mixed[:, 128 * q : 128 * q + 125], out)
    return out


def on_device(
    load_vector,
    fine_scale,
    coarse_scale,
    parent_owner,
    parent_pos,
    child_code,
    arrival_slot,
    fine_local,
    fine_left,
    fine_right,
    coarse_local,
    coarse_left,
    coarse_right,
):
    stiffness, extract, face_weight, face_diag, stiff_diag, upper_bound, halves, face_nodes = (
        element_tables()
    )
    pick = np.zeros((6, 125, 128))
    fold = np.zeros((6, 128, 125))
    weight = np.zeros((6, 128))
    for f in range(6):
        for m in range(25):
            pick[f, face_nodes[f, m], m] = 1.0
            fold[f, m, face_nodes[f, m]] = penalty_weight
            weight[f, m] = face_weight[f, m]
    prolong = np.zeros((125, 9 * 128))
    restrict = np.zeros((125, 9 * 128))
    for q in range(9):
        if q == 8:
            matrix = np.eye(125)
        else:
            matrix = np.kron(np.kron(halves[(q // 4) % 2], halves[(q // 2) % 2]), halves[q % 2])
        prolong[:, 128 * q : 128 * q + 125] = matrix.T
        restrict[:, 128 * q : 128 * q + 125] = matrix
    f32 = lambda a: jnp.asarray(a, jnp.float32)
    mats = (f32(stiffness.T), f32(pick), f32(fold), f32(weight))
    prolong = f32(prolong)
    restrict = f32(restrict)
    face_diag = f32(face_diag)
    stiff_diag = f32(stiff_diag)

    fine_plan = level_plan(fine_local, fine_left, fine_right)
    coarse_plan = level_plan(coarse_local, coarse_left, coarse_right)
    fine_col = fine_scale[:, None]
    coarse_col = coarse_scale[:, None]

    def fine_apply(vector_t):
        return apply_level(vector_t, fine_col, fine_plan, mats)

    def coarse_apply(vector_t):
        return apply_level(vector_t, coarse_col, coarse_plan, mats)

    def inverse_diagonal(scale_col):
        return 1.0 / (scale_col * stiff_diag[None, :] + penalty_weight * face_diag[None, :])

    fine_inverse = inverse_diagonal(fine_col)
    coarse_inverse = inverse_diagonal(coarse_col)
    load_t = load_vector.T
    first_x, first_r = chebyshev(
        jnp.zeros_like(load_t), load_t, fine_apply, fine_inverse, upper_bound, True
    )
    rank_count = lax.axis_size(AXES)
    slot_count = arrival_slot.shape[0]
    capacity = slot_count // rank_count
    coarse_count = coarse_scale.shape[0]
    target = parent_owner * capacity + parent_pos
    slot_ids = jnp.arange(slot_count, dtype=jnp.int32)
    coarse_ids = jnp.arange(coarse_count, dtype=jnp.int32)

    pieces = interpolate_t(first_r, child_code, restrict)
    buffer = place(onehot_of(slot_ids, target), pieces)
    arrived = lax.all_to_all(buffer, AXES, 0, 0, tiled=True)
    coarse_rhs = place(onehot_of(coarse_ids, arrival_slot), arrived)
    coarse_x, unused_r = chebyshev(
        jnp.zeros_like(coarse_rhs), coarse_rhs, coarse_apply, coarse_inverse, upper_bound, False
    )
    filled = place(onehot_of(arrival_slot, coarse_ids), coarse_x)
    returned = lax.all_to_all(filled, AXES, 0, 0, tiled=True)
    correction = interpolate_t(place(onehot_of(target, slot_ids), returned), child_code, prolong)
    second_x = first_x + correction
    second_r = first_r - fine_apply(correction)
    final_x, final_r = chebyshev(second_x, second_r, fine_apply, fine_inverse, upper_bound, True)
    return (final_x.T, final_r.T)


def solution(mesh):
    in_specs = (P(None, AXES),) + (P(AXES),) * 12
    out_specs = (P(None, AXES), P(None, AXES))
    return jax.shard_map(
        on_device, mesh=mesh, in_specs=in_specs, out_specs=out_specs, check_vma=False
    )
```

profile of v0, /device:TPU:2, one launch (start us, length us, event | category | flops | bytes accessed | tf_op | source)
XLA Modules:
  0.0 507.8 jit_solution(15623859705673203031)
XLA Ops:
  17.7 8.0 %collective-permute-start.1 = (f32[288,128]{1,0:T(8,128)}, f32[288,128]{1,0:T(8,128)}, u32[]{:S(2)}, u32[]{:S(2)}) collective-permute-start(f32[288,128]{1,0:T(8,128)} %get-tuple-element.67), channel_id=1, source_target_pairs={{1,0},{2,1},{3,2},{4,3},{5,4},{6,5},{7,6},{8,7},{9,8},{10,9},{11,1... | collective-permute-start | bytes 442376 | tf_op jit(solution)/shard_map/ppermute | solution.py:18
  29.2 14.8 %gather_fusion = f32[6912,128]{1,0:T(8,128)} fusion(f32[6912,128]{1,0:T(8,128)S(1)} %convolution_dynamic-update-slice_fusion.36, s32[7168]{0:T(1024)} %pad_clamp_fusion), kind=kCustom, calls=%fused_computation | custom fusion | bytes 7105536 | tf_op jit(solution)/shard_map/gather | solution.py:146
  70.9 7.9 %collective-permute-start.3 = (f32[288,128]{1,0:T(8,128)}, f32[288,128]{1,0:T(8,128)}, u32[]{:S(2)}, u32[]{:S(2)}) collective-permute-start(f32[288,128]{1,0:T(8,128)} %get-tuple-element.62), channel_id=1, source_target_pairs={{1,0},{2,1},{3,2},{4,3},{5,4},{6,5},{7,6},{8,7},{9,8},{10,9},{11,1... | collective-permute-start | bytes 442376 | tf_op jit(solution)/shard_map/ppermute | solution.py:18
  80.1 15.1 %gather_fusion.2 = f32[6912,128]{1,0:T(8,128)} fusion(f32[6912,128]{1,0:T(8,128)S(1)} %convolution_dynamic-update-slice_fusion.30, s32[7168]{0:T(1024)} %pad_clamp_fusion), kind=kCustom, calls=%fused_computation.2 | custom fusion | bytes 7105536 | tf_op jit(solution)/shard_map/gather | solution.py:146
  97.1 7.0 %fusion.5 = f32[6912,384]{1,0:T(8,128)S(1)} fusion(s32[576]{0:T(1024)} %pad_add_fusion, bf16[576,128]{1,0:T(8,128)(2,1)S(1)} %get-tuple-element.60, bf16[576,128]{1,0:T(8,128)(2,1)S(1)} %get-tuple-element.61, bf16[576,128]{1,0:T(8,128)(2,1)S(1)} %get-tuple-element.59), kind=kOutput, calls=%fused_computation.24 | convolution fusion | flops 3062956032 | bytes 11061504 | tf_op jit(solution)/shard_map/dot_general | solution.py:95
  123.1 7.9 %collective-permute-start.5 = (f32[288,128]{1,0:T(8,128)}, f32[288,128]{1,0:T(8,128)}, u32[]{:S(2)}, u32[]{:S(2)}) collective-permute-start(f32[288,128]{1,0:T(8,128)} %get-tuple-element.57), channel_id=1, source_target_pairs={{1,0},{2,1},{3,2},{4,3},{5,4},{6,5},{7,6},{8,7},{9,8},{10,9},{11,1... | collective-permute-start | bytes 442376 | tf_op jit(solution)/shard_map/ppermute | solution.py:18
  132.3 15.0 %gather_fusion.4 = f32[6912,128]{1,0:T(8,128)} fusion(f32[6912,128]{1,0:T(8,128)S(1)} %convolution_dynamic-update-slice_fusion.24, s32[7168]{0:T(1024)} %pad_clamp_fusion), kind=kCustom, calls=%fused_computation.4 | custom fusion | bytes 7105536 | tf_op jit(solution)/shard_map/gather | solution.py:146
  149.2 7.0 %fusion.4 = f32[6912,384]{1,0:T(8,128)S(1)} fusion(s32[576]{0:T(1024)} %pad_add_fusion, bf16[576,128]{1,0:T(8,128)(2,1)S(1)} %get-tuple-element.55, bf16[576,128]{1,0:T(8,128)(2,1)S(1)} %get-tuple-element.56, bf16[576,128]{1,0:T(8,128)(2,1)S(1)} %get-tuple-element.54), kind=kOutput, calls=%fused_computation.23 | convolution fusion | flops 3062956032 | bytes 11061504 | tf_op jit(solution)/shard_map/dot_general | solution.py:95
  181.8 24.3 %all-to-all-done = f32[128,18,125]{2,1,0:T(8,128)S(1)} async-done(((f32[128,18,125]{2,1,0:T(8,128)}), f32[128,18,125]{2,1,0:T(8,128)S(1)}, u32[]{:S(2)}, u32[]{:S(2)}) %all-to-all-start) | async-done | bytes 1152032 | tf_op jit(solution)/shard_map/all_to_all | solution.py:237
  212.2 7.8 %collective-permute-start.7 = (f32[64,128]{1,0:T(8,128)S(1)}, f32[64,128]{1,0:T(8,128)S(1)}, u32[]{:S(2)}, u32[]{:S(2)}) collective-permute-start(f32[64,128]{1,0:T(8,128)S(1)} %get-tuple-element.80), channel_id=1, source_target_pairs={{1,0},{2,1},{3,2},{4,3},{5,4},{6,5},{7,6},{8,7},{9,8},{10,9},{11,1... | collective-permute-start | bytes 98312 | tf_op jit(solution)/shard_map/ppermute | solution.py:18
  231.7 8.0 %collective-permute-start.9 = (f32[64,128]{1,0:T(8,128)S(1)}, f32[64,128]{1,0:T(8,128)S(1)}, u32[]{:S(2)}, u32[]{:S(2)}) collective-permute-start(f32[64,128]{1,0:T(8,128)S(1)} %get-tuple-element.75), channel_id=1, source_target_pairs={{1,0},{2,1},{3,2},{4,3},{5,4},{6,5},{7,6},{8,7},{9,8},{10,9},{11,1... | collective-permute-start | bytes 98312 | tf_op jit(solution)/shard_map/ppermute | solution.py:18
  244.5 33.0 %all_to_all.24 = f32[128,18,125]{2,1,0:T(8,128)S(1)} all-to-all(f32[128,18,125]{2,1,0:T(8,128)S(1)} %all_to_all.19), channel_id=1, replica_groups=mesh['elem'=16,'sub'=8] {'elem','sub'}, dimensions={0} | all-to-all | bytes 2304000 | tf_op jit(solution)/shard_map/all_to_all | solution.py:243
  299.0 7.9 %collective-permute-start.11 = (f32[288,128]{1,0:T(8,128)}, f32[288,128]{1,0:T(8,128)}, u32[]{:S(2)}, u32[]{:S(2)}) collective-permute-start(f32[288,128]{1,0:T(8,128)} %get-tuple-element.52), channel_id=1, source_target_pairs={{1,0},{2,1},{3,2},{4,3},{5,4},{6,5},{7,6},{8,7},{9,8},{10,9},{11,1... | collective-permute-start | bytes 442376 | tf_op jit(solution)/shard_map/ppermute | solution.py:18
  306.9 14.8 %gather_fusion.10 = f32[6912,128]{1,0:T(8,128)} fusion(f32[6912,128]{1,0:T(8,128)S(1)} %convolution_dynamic-update-slice_fusion.18, s32[7168]{0:T(1024)} %pad_clamp_fusion), kind=kCustom, calls=%fused_computation.10 | custom fusion | bytes 7105536 | tf_op jit(solution)/shard_map/gather | solution.py:146
  323.6 7.0 %fusion.3 = f32[6912,384]{1,0:T(8,128)S(1)} fusion(s32[576]{0:T(1024)} %pad_add_fusion, bf16[576,128]{1,0:T(8,128)(2,1)S(1)} %get-tuple-element.50, bf16[576,128]{1,0:T(8,128)(2,1)S(1)} %get-tuple-element.51, bf16[576,128]{1,0:T(8,128)(2,1)S(1)} %get-tuple-element.49), kind=kOutput, calls=%fused_computation.22 | convolution fusion | flops 3062956032 | bytes 11061504 | tf_op jit(solution)/shard_map/dot_general | solution.py:95
  350.0 7.9 %collective-permute-start.13 = (f32[288,128]{1,0:T(8,128)}, f32[288,128]{1,0:T(8,128)}, u32[]{:S(2)}, u32[]{:S(2)}) collective-permute-start(f32[288,128]{1,0:T(8,128)} %get-tuple-element.47), channel_id=1, source_target_pairs={{1,0},{2,1},{3,2},{4,3},{5,4},{6,5},{7,6},{8,7},{9,8},{10,9},{11,1... | collective-permute-start | bytes 442376 | tf_op jit(solution)/shard_map/ppermute | solution.py:18
  357.9 15.0 %gather_fusion.12 = f32[6912,128]{1,0:T(8,128)} fusion(f32[6912,128]{1,0:T(8,128)S(1)} %convolution_dynamic-update-slice_fusion.12, s32[7168]{0:T(1024)} %pad_clamp_fusion), kind=kCustom, calls=%fused_computation.12 | custom fusion | bytes 7105536 | tf_op jit(solution)/shard_map/gather | solution.py:146
  374.8 7.0 %fusion.2 = f32[6912,384]{1,0:T(8,128)S(1)} fusion(s32[576]{0:T(1024)} %pad_add_fusion, bf16[576,128]{1,0:T(8,128)(2,1)S(1)} %get-tuple-element.45, bf16[576,128]{1,0:T(8,128)(2,1)S(1)} %get-tuple-element.46, bf16[576,128]{1,0:T(8,128)(2,1)S(1)} %get-tuple-element.44), kind=kOutput, calls=%fused_computation.21 | convolution fusion | flops 3062956032 | bytes 11061504 | tf_op jit(solution)/shard_map/dot_general | solution.py:95
  400.8 7.9 %collective-permute-start.15 = (f32[288,128]{1,0:T(8,128)}, f32[288,128]{1,0:T(8,128)}, u32[]{:S(2)}, u32[]{:S(2)}) collective-permute-start(f32[288,128]{1,0:T(8,128)} %get-tuple-element.42), channel_id=1, source_target_pairs={{1,0},{2,1},{3,2},{4,3},{5,4},{6,5},{7,6},{8,7},{9,8},{10,9},{11,1... | collective-permute-start | bytes 442376 | tf_op jit(solution)/shard_map/ppermute | solution.py:18
  408.7 15.1 %gather_fusion.14 = f32[6912,128]{1,0:T(8,128)} fusion(f32[6912,128]{1,0:T(8,128)S(1)} %convolution_dynamic-update-slice_fusion.6, s32[7168]{0:T(1024)} %pad_clamp_fusion), kind=kCustom, calls=%fused_computation.14 | custom fusion | bytes 7105536 | tf_op jit(solution)/shard_map/gather | solution.py:146
  425.8 7.0 %fusion.1 = f32[6912,384]{1,0:T(8,128)S(1)} fusion(s32[576]{0:T(1024)} %pad_add_fusion, bf16[576,128]{1,0:T(8,128)(2,1)S(1)} %get-tuple-element.40, bf16[576,128]{1,0:T(8,128)(2,1)S(1)} %get-tuple-element.41, bf16[576,128]{1,0:T(8,128)(2,1)S(1)} %get-tuple-element.39), kind=kOutput, calls=%fused_computation.20 | convolution fusion | flops 3062956032 | bytes 11061504 | tf_op jit(solution)/shard_map/dot_general | solution.py:95
  440.9 15.0 %add_bitcast_fusion = (f32[125,1152]{0,1:T(8,128)}, f32[1152,125]{1,0:T(8,128)S(1)}) fusion(f32[1152,125]{1,0:T(8,128)S(1)} %copy-done.12, f32[1152,125]{1,0:T(8,128)S(1)} %copy-done.3, f32[1152,125]{1,0:T(8,128)S(1)} %copy-done.10, f32[125,1152]{0,1:T(8,128)S(1)} %copy-done.25, f32[125]{0:T(128)S(1)} %copy-done.143, f32[125]{0:T(128)S(1)} %copy-done.152, ...), kind=kLoop, calls=%fused_computation.283 | loop fusion | flops 3888000 | bytes 10383976 | tf_op jit(solution)/shard_map/transpose | solution.py:248
  465.6 7.9 %collective-permute-start.17 = (f32[288,128]{1,0:T(8,128)}, f32[288,128]{1,0:T(8,128)}, u32[]{:S(2)}, u32[]{:S(2)}) collective-permute-start(f32[288,128]{1,0:T(8,128)} %get-tuple-element.37), channel_id=1, source_target_pairs={{1,0},{2,1},{3,2},{4,3},{5,4},{6,5},{7,6},{8,7},{9,8},{10,9},{11,1... | collective-permute-start | bytes 442376 | tf_op jit(solution)/shard_map/ppermute | solution.py:18
  473.5 14.8 %gather_fusion.16 = f32[6912,128]{1,0:T(8,128)} fusion(f32[6912,128]{1,0:T(8,128)S(1)} %convolution_dynamic-update-slice_fusion, s32[7168]{0:T(1024)} %pad_clamp_fusion), kind=kCustom, calls=%fused_computation.16 | custom fusion | bytes 7105536 | tf_op jit(solution)/shard_map/gather | solution.py:146
  (527 shorter events, 220.4 us)
Async XLA Ops:
  10.3 17.6 %copy-start.136 = (s32[288]{0:T(512)S(1)}, s32[288]{0:T(512)}, u32[]{:S(2)}) copy-start(s32[288]{0:T(512)} %param.30) | copy-start | bytes 3460
  15.8 28.2 %collective-permute-start = (f32[288,128]{1,0:T(8,128)}, f32[288,128]{1,0:T(8,128)}, u32[]{:S(2)}, u32[]{:S(2)}) collective-permute-start(f32[288,128]{1,0:T(8,128)} %get-tuple-element.68), channel_id=1, source_target_pairs={{0,1},{1,2},{2,3},{3,4},{4,5},{5,6},{6,7},{7,8},{8,9},{9,10},{10,1... | collective-permute-start | bytes 442376 | tf_op jit(solution)/shard_map/ppermute | solution.py:18
  17.7 27.2 %collective-permute-start.1 = (f32[288,128]{1,0:T(8,128)}, f32[288,128]{1,0:T(8,128)}, u32[]{:S(2)}, u32[]{:S(2)}) collective-permute-start(f32[288,128]{1,0:T(8,128)} %get-tuple-element.67), channel_id=1, source_target_pairs={{1,0},{2,1},{3,2},{4,3},{5,4},{6,5},{7,6},{8,7},{9,8},{10,9},{11,1... | collective-permute-start | bytes 442376 | tf_op jit(solution)/shard_map/ppermute | solution.py:18
  29.2 16.8 %copy-start.153 = (s32[576]{0:T(1024)S(1)}, s32[576]{0:T(1024)}, u32[]{:S(2)}) copy-start(s32[576]{0:T(1024)} %pad_add_fusion) | copy-start | bytes 6916
  69.0 26.2 %collective-permute-start.2 = (f32[288,128]{1,0:T(8,128)}, f32[288,128]{1,0:T(8,128)}, u32[]{:S(2)}, u32[]{:S(2)}) collective-permute-start(f32[288,128]{1,0:T(8,128)} %get-tuple-element.63), channel_id=1, source_target_pairs={{0,1},{1,2},{2,3},{3,4},{4,5},{5,6},{6,7},{7,8},{8,9},{9,10},{10,1... | collective-permute-start | bytes 442376 | tf_op jit(solution)/shard_map/ppermute | solution.py:18
  70.9 25.2 %collective-permute-start.3 = (f32[288,128]{1,0:T(8,128)}, f32[288,128]{1,0:T(8,128)}, u32[]{:S(2)}, u32[]{:S(2)}) collective-permute-start(f32[288,128]{1,0:T(8,128)} %get-tuple-element.62), channel_id=1, source_target_pairs={{1,0},{2,1},{3,2},{4,3},{5,4},{6,5},{7,6},{8,7},{9,8},{10,9},{11,1... | collective-permute-start | bytes 442376 | tf_op jit(solution)/shard_map/ppermute | solution.py:18
  121.2 26.1 %collective-permute-start.4 = (f32[288,128]{1,0:T(8,128)}, f32[288,128]{1,0:T(8,128)}, u32[]{:S(2)}, u32[]{:S(2)}) collective-permute-start(f32[288,128]{1,0:T(8,128)} %get-tuple-element.58), channel_id=1, source_target_pairs={{0,1},{1,2},{2,3},{3,4},{4,5},{5,6},{6,7},{7,8},{8,9},{9,10},{10,1... | collective-permute-start | bytes 442376 | tf_op jit(solution)/shard_map/ppermute | solution.py:18
  123.1 25.1 %collective-permute-start.5 = (f32[288,128]{1,0:T(8,128)}, f32[288,128]{1,0:T(8,128)}, u32[]{:S(2)}, u32[]{:S(2)}) collective-permute-start(f32[288,128]{1,0:T(8,128)} %get-tuple-element.57), channel_id=1, source_target_pairs={{1,0},{2,1},{3,2},{4,3},{5,4},{6,5},{7,6},{8,7},{9,8},{10,9},{11,1... | collective-permute-start | bytes 442376 | tf_op jit(solution)/shard_map/ppermute | solution.py:18
  177.3 28.8 %all-to-all-start = ((f32[128,18,125]{2,1,0:T(8,128)}), f32[128,18,125]{2,1,0:T(8,128)S(1)}, u32[]{:S(2)}, u32[]{:S(2)}) async-start(f32[128,18,125]{2,1,0:T(8,128)} %all_to_all.16), calls=%async_computation | async-start | bytes 3145728 | tf_op jit(solution)/shard_map/all_to_all | solution.py:237
  181.8 24.8 %copy-start.133 = (s32[2304]{0:T(1024)S(1)}, s32[2304]{0:T(1024)}, u32[]{:S(2)}) copy-start(s32[2304]{0:T(1024)} %param.27) | copy-start | bytes 27652
  210.1 12.5 %collective-permute-start.6 = (f32[64,128]{1,0:T(8,128)S(1)}, f32[64,128]{1,0:T(8,128)S(1)}, u32[]{:S(2)}, u32[]{:S(2)}) collective-permute-start(f32[64,128]{1,0:T(8,128)S(1)} %get-tuple-element.81), channel_id=1, source_target_pairs={{0,1},{1,2},{2,3},{3,4},{4,5},{5,6},{6,7},{7,8},{8,9},{9,10},{10,1... | collective-permute-start | bytes 98312 | tf_op jit(solution)/shard_map/ppermute | solution.py:18
  212.2 10.5 %collective-permute-start.7 = (f32[64,128]{1,0:T(8,128)S(1)}, f32[64,128]{1,0:T(8,128)S(1)}, u32[]{:S(2)}, u32[]{:S(2)}) collective-permute-start(f32[64,128]{1,0:T(8,128)S(1)} %get-tuple-element.80), channel_id=1, source_target_pairs={{1,0},{2,1},{3,2},{4,3},{5,4},{6,5},{7,6},{8,7},{9,8},{10,9},{11,1... | collective-permute-start | bytes 98312 | tf_op jit(solution)/shard_map/ppermute | solution.py:18
  227.2 12.6 %collective-permute-start.8 = (f32[64,128]{1,0:T(8,128)S(1)}, f32[64,128]{1,0:T(8,128)S(1)}, u32[]{:S(2)}, u32[]{:S(2)}) collective-permute-start(f32[64,128]{1,0:T(8,128)S(1)} %get-tuple-element.76), channel_id=1, source_target_pairs={{0,1},{1,2},{2,3},{3,4},{4,5},{5,6},{6,7},{7,8},{8,9},{9,10},{10,1... | collective-permute-start | bytes 98312 | tf_op jit(solution)/shard_map/ppermute | solution.py:18
  231.7 9.4 %collective-permute-start.9 = (f32[64,128]{1,0:T(8,128)S(1)}, f32[64,128]{1,0:T(8,128)S(1)}, u32[]{:S(2)}, u32[]{:S(2)}) collective-permute-start(f32[64,128]{1,0:T(8,128)S(1)} %get-tuple-element.75), channel_id=1, source_target_pairs={{1,0},{2,1},{3,2},{4,3},{5,4},{6,5},{7,6},{8,7},{9,8},{10,9},{11,1... | collective-permute-start | bytes 98312 | tf_op jit(solution)/shard_map/ppermute | solution.py:18
  297.1 24.6 %collective-permute-start.10 = (f32[288,128]{1,0:T(8,128)}, f32[288,128]{1,0:T(8,128)}, u32[]{:S(2)}, u32[]{:S(2)}) collective-permute-start(f32[288,128]{1,0:T(8,128)} %get-tuple-element.53), channel_id=1, source_target_pairs={{0,1},{1,2},{2,3},{3,4},{4,5},{5,6},{6,7},{7,8},{8,9},{9,10},{10,1... | collective-permute-start | bytes 442376 | tf_op jit(solution)/shard_map/ppermute | solution.py:18
  299.0 23.6 %collective-permute-start.11 = (f32[288,128]{1,0:T(8,128)}, f32[288,128]{1,0:T(8,128)}, u32[]{:S(2)}, u32[]{:S(2)}) collective-permute-start(f32[288,128]{1,0:T(8,128)} %get-tuple-element.52), channel_id=1, source_target_pairs={{1,0},{2,1},{3,2},{4,3},{5,4},{6,5},{7,6},{8,7},{9,8},{10,9},{11,1... | collective-permute-start | bytes 442376 | tf_op jit(solution)/shard_map/ppermute | solution.py:18
  348.1 24.8 %collective-permute-start.12 = (f32[288,128]{1,0:T(8,128)}, f32[288,128]{1,0:T(8,128)}, u32[]{:S(2)}, u32[]{:S(2)}) collective-permute-start(f32[288,128]{1,0:T(8,128)} %get-tuple-element.48), channel_id=1, source_target_pairs={{0,1},{1,2},{2,3},{3,4},{4,5},{5,6},{6,7},{7,8},{8,9},{9,10},{10,1... | collective-permute-start | bytes 442376 | tf_op jit(solution)/shard_map/ppermute | solution.py:18
  350.0 23.8 %collective-permute-start.13 = (f32[288,128]{1,0:T(8,128)}, f32[288,128]{1,0:T(8,128)}, u32[]{:S(2)}, u32[]{:S(2)}) collective-permute-start(f32[288,128]{1,0:T(8,128)} %get-tuple-element.47), channel_id=1, source_target_pairs={{1,0},{2,1},{3,2},{4,3},{5,4},{6,5},{7,6},{8,7},{9,8},{10,9},{11,1... | collective-permute-start | bytes 442376 | tf_op jit(solution)/shard_map/ppermute | solution.py:18
  398.9 24.9 %collective-permute-start.14 = (f32[288,128]{1,0:T(8,128)}, f32[288,128]{1,0:T(8,128)}, u32[]{:S(2)}, u32[]{:S(2)}) collective-permute-start(f32[288,128]{1,0:T(8,128)} %get-tuple-element.43), channel_id=1, source_target_pairs={{0,1},{1,2},{2,3},{3,4},{4,5},{5,6},{6,7},{7,8},{8,9},{9,10},{10,1... | collective-permute-start | bytes 442376 | tf_op jit(solution)/shard_map/ppermute | solution.py:18
  400.8 23.9 %collective-permute-start.15 = (f32[288,128]{1,0:T(8,128)}, f32[288,128]{1,0:T(8,128)}, u32[]{:S(2)}, u32[]{:S(2)}) collective-permute-start(f32[288,128]{1,0:T(8,128)} %get-tuple-element.42), channel_id=1, source_target_pairs={{1,0},{2,1},{3,2},{4,3},{5,4},{6,5},{7,6},{8,7},{9,8},{10,9},{11,1... | collective-permute-start | bytes 442376 | tf_op jit(solution)/shard_map/ppermute | solution.py:18
  440.9 16.3 %copy-start.74 = (f32[125,128]{1,0:T(8,128)S(1)}, f32[125,128]{1,0:T(8,128)}, u32[]{:S(2)}) copy-start(f32[125,128]{1,0:T(8,128)} %constant.120) | copy-start | bytes 192004
  463.7 26.7 %collective-permute-start.16 = (f32[288,128]{1,0:T(8,128)}, f32[288,128]{1,0:T(8,128)}, u32[]{:S(2)}, u32[]{:S(2)}) collective-permute-start(f32[288,128]{1,0:T(8,128)} %get-tuple-element.38), channel_id=1, source_target_pairs={{0,1},{1,2},{2,3},{3,4},{4,5},{5,6},{6,7},{7,8},{8,9},{9,10},{10,1... | collective-permute-start | bytes 442376 | tf_op jit(solution)/shard_map/ppermute | solution.py:18
  465.6 26.8 %copy-start.154 = (s32[576]{0:T(1024)S(1)}, s32[576]{0:T(1024)}, u32[]{:S(2)}) copy-start(s32[576]{0:T(1024)} %pad_add_fusion) | copy-start | bytes 6916
  465.6 25.7 %collective-permute-start.17 = (f32[288,128]{1,0:T(8,128)}, f32[288,128]{1,0:T(8,128)}, u32[]{:S(2)}, u32[]{:S(2)}) collective-permute-start(f32[288,128]{1,0:T(8,128)} %get-tuple-element.37), channel_id=1, source_target_pairs={{1,0},{2,1},{3,2},{4,3},{5,4},{6,5},{7,6},{8,7},{9,8},{10,9},{11,1... | collective-permute-start | bytes 442376 | tf_op jit(solution)/shard_map/ppermute | solution.py:18
  (158 other events, 602.5 us)
where the time goes:
time: 511 us; the launch traced here: 508 us
  local copies, waits for them, and re-layouts  163 us (32%)
  matrix products  130 us (25%)
  starting transfers between devices  92.7 us (18%)
  other arithmetic  58.8 us (12%)
  blocking collectives  33 us (6%)
  waiting for transfers between devices  25.8 us (5%)
    gather x9, local copies, waits for them, and re-layouts, apply_level(): partner = jnp.where(has_local[:, None], faces[source], 0.0)  110 us
    ppermute x18, starting transfers between devices, passed_along(): return lax.ppermute(block, axis, route)  88.3 us
    dot_general x13, matrix products, place(): jnp.dot(onehot, jnp.concatenate(parts, axis=1), preferred_element_type=jn...  55.8 us
    all_to_all x1, blocking collectives, on_device(): returned = lax.all_to_all(filled, AXES, 0, 0, tiled=True)  33 us
    dot_general x54, matrix products, apply_level(): jnp.dot(vector_t, pick[f], precision=highest)  32.4 us
    sub x9, other arithmetic, apply_level(): jump = (faces - partner).reshape(6, elem_count, 128) * weight[:, None, :]  30.1 us
    all_to_all x1, waiting for transfers between devices, on_device(): arrived = lax.all_to_all(buffer, AXES, 0, 0, tiled=True)  24.3 us
    dot_general x9, matrix products, apply_level(): lax.dot_general(jump, fold, (((2,), (1,)), ((0,), (0,))), precision=highest)  22.2 us
  transfers between devices with their start and end apart: 19, of which 2 were waited for; matrix products, arithmetic and copies ran while one was open for 25% of the time, Pallas kernels for 0%

commit v1 on v0

--- a/solution.py
+++ b/solution.py
@@ -123,18 +123,30 @@
     return (rows_ids[:, None] == column_ids[None, :]).astype(jnp.bfloat16)
 
 
-def level_plan(local_ids, left_ids, right_ids):
+def level_plan(local_ids, left_ids, right_ids, weight):
     face_count = local_ids.shape[0]
+    elem_count = face_count // 6
     has_local = local_ids >= 0
     source = jnp.where(has_local, local_ids, 0)
     send_ids = jnp.concatenate([left_ids, right_ids])
     onehot = onehot_of(jnp.arange(face_count, dtype=jnp.int32), send_ids)
-    return has_local, source, send_ids, onehot
+    face_w = jnp.broadcast_to(weight[:, None, :], (6, elem_count, 25)).reshape(face_count, 25)
+    local_w = jnp.where(has_local[:, None], face_w, 0.0)
+    return source, send_ids, onehot, face_w, local_w
+
+
+def place_packed(onehot, values):
+    high, middle, low = split3(values[:, :25])
+    gap = jnp.zeros((values.shape[0], 7), jnp.bfloat16)
+    tail = jnp.zeros((values.shape[0], 39), jnp.bfloat16)
+    packed = jnp.concatenate([high, gap, middle, gap, low, tail], axis=1)
+    out = jnp.dot(onehot, packed, preferred_element_type=jnp.float32)
+    return (out[:, 0:25] + out[:, 32:57]) + out[:, 64:89]
 
 
 def apply_level(vector_t, scale_col, plan, mats):
-    has_local, source, send_ids, onehot = plan
-    stiffness_t, pick, fold, weight = mats
+    source, send_ids, onehot, face_w, local_w = plan
+    stiffness_t, pick, fold = mats
     elem_count = vector_t.shape[0]
     shared = send_ids.shape[0] // 2
     faces = jnp.concatenate(
@@ -143,12 +155,12 @@
     sent = faces[send_ids]
     from_left = passed_along(sent[shared:], AXES, 1)
     from_right = passed_along(sent[:shared], AXES, -1)
-    partner = jnp.where(has_local[:, None], faces[source], 0.0)
+    local = faces[source]
     received = jnp.concatenate([from_left, from_right], axis=0)
-    partner = partner + place(onehot, received)
-    jump = (faces - partner).reshape(6, elem_count, 128) * weight[:, None, :]
+    boundary = place_packed(onehot, received)
+    jump = (faces[:, :25] - boundary) * face_w - local[:, :25] * local_w
     folded = lax.dot_general(
-        jump, fold, (((2,), (1,)), ((0,), (0,))), precision=highest
+        jump.reshape(6, elem_count, 25), fold, (((2,), (1,)), ((0,), (0,))), precision=highest
     ).sum(axis=0)
     interior = scale_col * jnp.dot(vector_t, stiffness_t, precision=highest)
     return interior + folded
@@ -181,8 +193,8 @@
         element_tables()
     )
     pick = np.zeros((6, 125, 128))
-    fold = np.zeros((6, 128, 125))
-    weight = np.zeros((6, 128))
+    fold = np.zeros((6, 25, 125))
+    weight = np.zeros((6, 25))
     for f in range(6):
         for m in range(25):
             pick[f, face_nodes[f, m], m] = 1.0
@@ -198,14 +210,15 @@
         prolong[:, 128 * q : 128 * q + 125] = matrix.T
         restrict[:, 128 * q : 128 * q + 125] = matrix
     f32 = lambda a: jnp.asarray(a, jnp.float32)
-    mats = (f32(stiffness.T), f32(pick), f32(fold), f32(weight))
+    mats = (f32(stiffness.T), f32(pick), f32(fold))
+    weight = f32(weight)
     prolong = f32(prolong)
     restrict = f32(restrict)
     face_diag = f32(face_diag)
     stiff_diag = f32(stiff_diag)
 
-    fine_plan = level_plan(fine_local, fine_left, fine_right)
-    coarse_plan = level_plan(coarse_local, coarse_left, coarse_right)
+    fine_plan = level_plan(fine_local, fine_left, fine_right, weight)
+    coarse_plan = level_plan(coarse_local, coarse_left, coarse_right, weight)
     fine_col = fine_scale[:, None]
     coarse_col = coarse_scale[:, None]
 

time: 511 us -> 613 us (1.20); the launches traced: 508 us -> 602 us
  local copies, waits for them, and re-layouts: 163 us -> 225 us
  other arithmetic: 58.8 us -> 84.4 us
  matrix products: 130 us -> 143 us
  starting transfers between devices: 92.7 us -> 82.9 us
  waiting for transfers between devices: 25.8 us -> 34.6 us
    dot_general x9 -> x18, matrix products: 22.2 us -> 82 us  [the longest x9 43.6 us: place_packed(): out = jnp.dot(onehot, packed, preferred_element_type=jnp.float32)]
    dot_general x13 -> x4, matrix products: 55.8 us -> 7.69 us  [place(): jnp.dot(onehot, jnp.concatenate(parts, axis=1), preferred_element_type=jn...]
    convert_element_type x0 -> x27, local copies, waits for them, and re-layouts: none -> 33.8 us  [split3(): return tuple((part.astype(jnp.bfloat16) for part in (high, middle, low)))]
    sub x9, other arithmetic: 30.1 us -> 51.6 us  [apply_level(): jump = (faces[:, :25] - boundary) * face_w - local[:, :25] * local_w]
    unnamed x338 -> x319, local copies, waits for them, and re-layouts: 14.1 us -> 31.8 us
    ppermute x18, starting transfers between devices: 88.3 us -> 73.1 us  [passed_along(): return lax.ppermute(block, axis, route)]
    convert_element_type x13 -> x22, other arithmetic: 3.95 us -> 18.3 us  [split3(): return tuple((part.astype(jnp.bfloat16) for part in (high, middle, low)))]
    transpose x1, other arithmetic: 15 us -> 4.22 us  [on_device(): return (final_x.T, final_r.T)]
  transfers between devices with their start and end apart: 19 -> 19, of which waited for: 2 -> 3; matrix products, arithmetic and copies ran while one was open for 25% -> 20% of each run, Pallas kernels for 0% -> 0%
where the time goes in v1:
time: 613 us; the launch traced here: 602 us
  local copies, waits for them, and re-layouts  225 us (37%)
  matrix products  143 us (23%)
  other arithmetic  84.4 us (14%)
  starting transfers between devices  82.9 us (14%)
  waiting for transfers between devices  34.6 us (6%)
  blocking collectives  28 us (5%)
    gather x9, local copies, waits for them, and re-layouts, apply_level(): local = faces[source]  110 us
    ppermute x18, starting transfers between devices, passed_along(): return lax.ppermute(block, axis, route)  73.1 us
    sub x9, other arithmetic, apply_level(): jump = (faces[:, :25] - boundary) * face_w - local[:, :25] * local_w  51.6 us
    dot_general x9, matrix products, place_packed(): out = jnp.dot(onehot, packed, preferred_element_type=jnp.float32)  43.6 us
    dot_general x9, matrix products, apply_level(): lax.dot_general(jump.reshape(6, elem_count, 25), fold, (((2,), (1,)), ((0...  38.4 us
    convert_element_type x27, local copies, waits for them, and re-layouts, split3(): return tuple((part.astype(jnp.bfloat16) for part in (high, middle, low)))  33.8 us
    dot_general x54, matrix products, apply_level(): jnp.dot(vector_t, pick[f], precision=highest)  32.6 us
    unnamed x319, local copies, waits for them, and re-layouts  31.8 us
  transfers between devices with their start and end apart: 19, of which 3 were waited for; matrix products, arithmetic and copies ran while one was open for 20% of the time, Pallas kernels for 0%

profile of v1, /device:TPU:2, one launch (start us, length us, event | category | flops | bytes accessed | tf_op | source)
XLA Modules:
  0.0 601.6 jit_solution(17710986652878754217)
XLA Ops:
  18.1 7.8 %collective-permute-start.1 = (f32[288,128]{0,1:T(8,128)}, f32[288,128]{0,1:T(8,128)}, u32[]{:S(2)}, u32[]{:S(2)}) collective-permute-start(f32[288,128]{0,1:T(8,128)} %copy.306), channel_id=1, source_target_pairs={{1,0},{2,1},{3,2},{4,3},{5,4},{6,5},{7,6},{8,7},{9,8},{10,9},{11,1... | collective-permute-start | bytes 442376 | tf_op jit(solution)/shard_map/ppermute | solution.py:18
  31.6 15.1 %gather_fusion.1 = f32[6912,128]{1,0:T(8,128)} fusion(f32[6912,128]{1,0:T(8,128)S(1)} %convolution_dynamic-update-slice_fusion.36, s32[7168]{0:T(1024)} %pad_clamp_fusion), kind=kCustom, calls=%fused_computation.1 | custom fusion | bytes 7105536 | tf_op jit(solution)/shard_map/gather | solution.py:158
  64.5 6.8 %fusion.25 = f32[6912,25]{1,0:T(8,128)} fusion(f32[6912,128]{1,0:T(8,128)} %gather_fusion.1, f32[6912,128]{1,0:T(8,128)S(1)} %fusion.6, f32[6912,128]{1,0:T(8,128)S(1)} %convolution_dynamic-update-slice_fusion.36, f32[6,25]{1,0:T(8,128)S(1)} %copy-done.98, pred[6912]{0:T(1024)(128)(4,1)S(1)} %broadcast_compare_fusion), kind=kLoop, calls=%fused_computation.56 | loop fusion | flops 1209600 | bytes 4154712 | tf_op jit(solution)/shard_map/sub | solution.py:161
  89.9 7.9 %collective-permute-start.3 = (f32[288,128]{0,1:T(8,128)}, f32[288,128]{0,1:T(8,128)}, u32[]{:S(2)}, u32[]{:S(2)}) collective-permute-start(f32[288,128]{0,1:T(8,128)} %copy.308), channel_id=1, source_target_pairs={{1,0},{2,1},{3,2},{4,3},{5,4},{6,5},{7,6},{8,7},{9,8},{10,9},{11,1... | collective-permute-start | bytes 442376 | tf_op jit(solution)/shard_map/ppermute | solution.py:18
  101.0 14.8 %gather_fusion.3 = f32[6912,128]{1,0:T(8,128)} fusion(f32[6912,128]{1,0:T(8,128)S(1)} %convolution_dynamic-update-slice_fusion.30, s32[7168]{0:T(1024)} %pad_clamp_fusion), kind=kCustom, calls=%fused_computation.3 | custom fusion | bytes 7105536 | tf_op jit(solution)/shard_map/gather | solution.py:158
  130.8 6.8 %fusion.26 = f32[6912,25]{1,0:T(8,128)} fusion(f32[6912,128]{1,0:T(8,128)} %gather_fusion.3, f32[6912,128]{1,0:T(8,128)S(1)} %fusion.5, f32[6912,128]{1,0:T(8,128)S(1)} %convolution_dynamic-update-slice_fusion.30, f32[6,25]{1,0:T(8,128)S(1)} %copy-done.98, pred[6912]{0:T(1024)(128)(4,1)S(1)} %broadcast_compare_fusion), kind=kLoop, calls=%fused_computation.57 | loop fusion | flops 1209600 | bytes 4154712 | tf_op jit(solution)/shard_map/sub | solution.py:161
  155.9 7.9 %collective-permute-start.5 = (f32[288,128]{0,1:T(8,128)}, f32[288,128]{0,1:T(8,128)}, u32[]{:S(2)}, u32[]{:S(2)}) collective-permute-start(f32[288,128]{0,1:T(8,128)} %copy.310), channel_id=1, source_target_pairs={{1,0},{2,1},{3,2},{4,3},{5,4},{6,5},{7,6},{8,7},{9,8},{10,9},{11,1... | collective-permute-start | bytes 442376 | tf_op jit(solution)/shard_map/ppermute | solution.py:18
  167.0 14.8 %gather_fusion.5 = f32[6912,128]{1,0:T(8,128)} fusion(f32[6912,128]{1,0:T(8,128)S(1)} %convolution_dynamic-update-slice_fusion.24, s32[7168]{0:T(1024)} %pad_clamp_fusion), kind=kCustom, calls=%fused_computation.5 | custom fusion | bytes 7105536 | tf_op jit(solution)/shard_map/gather | solution.py:158
  196.8 6.8 %fusion.27 = f32[6912,25]{1,0:T(8,128)} fusion(f32[6912,128]{1,0:T(8,128)} %gather_fusion.5, f32[6912,128]{1,0:T(8,128)S(1)} %fusion.4, f32[6912,128]{1,0:T(8,128)S(1)} %convolution_dynamic-update-slice_fusion.24, f32[6,25]{1,0:T(8,128)S(1)} %copy-done.98, pred[6912]{0:T(1024)(128)(4,1)S(1)} %broadcast_compare_fusion), kind=kLoop, calls=%fused_computation.58 | loop fusion | flops 1209600 | bytes 4154712 | tf_op jit(solution)/shard_map/sub | solution.py:161
  222.7 9.8 %all-to-all-start = ((f32[128,18,125]{2,1,0:T(8,128)}), f32[128,18,125]{2,1,0:T(8,128)S(1)}, u32[]{:S(2)}, u32[]{:S(2)}) async-start(f32[128,18,125]{2,1,0:T(8,128)} %all_to_all.16), calls=%async_computation | async-start | bytes 3145728 | tf_op jit(solution)/shard_map/all_to_all | solution.py:250
  232.6 24.3 %all-to-all-done = f32[128,18,125]{2,1,0:T(8,128)S(1)} async-done(((f32[128,18,125]{2,1,0:T(8,128)}), f32[128,18,125]{2,1,0:T(8,128)S(1)}, u32[]{:S(2)}, u32[]{:S(2)}) %all-to-all-start) | async-done | bytes 1152032 | tf_op jit(solution)/shard_map/all_to_all | solution.py:250
  295.9 28.0 %all_to_all.24 = f32[128,18,125]{2,1,0:T(8,128)S(1)} all-to-all(f32[128,18,125]{2,1,0:T(8,128)S(1)} %all_to_all.19), channel_id=1, replica_groups=mesh['elem'=16,'sub'=8] {'elem','sub'}, dimensions={0} | all-to-all | bytes 2304000 | tf_op jit(solution)/shard_map/all_to_all | solution.py:256
  351.2 15.2 %gather_fusion.11 = f32[6912,128]{1,0:T(8,128)} fusion(f32[6912,128]{1,0:T(8,128)S(1)} %convolution_dynamic-update-slice_fusion.18, s32[7168]{0:T(1024)} %pad_clamp_fusion), kind=kCustom, calls=%fused_computation.11 | custom fusion | bytes 7105536 | tf_op jit(solution)/shard_map/gather | solution.py:158
  381.5 6.7 %fusion.28 = f32[6912,25]{1,0:T(8,128)} fusion(f32[6912,128]{1,0:T(8,128)} %gather_fusion.11, f32[6912,128]{1,0:T(8,128)S(1)} %fusion.3, f32[6912,128]{1,0:T(8,128)S(1)} %convolution_dynamic-update-slice_fusion.18, f32[6,25]{1,0:T(8,128)S(1)} %copy-done.98, pred[6912]{0:T(1024)(128)(4,1)S(1)} %broadcast_compare_fusion), kind=kLoop, calls=%fused_computation.59 | loop fusion | flops 1209600 | bytes 4154712 | tf_op jit(solution)/shard_map/sub | solution.py:161
  407.1 7.9 %collective-permute-start.13 = (f32[288,128]{0,1:T(8,128)}, f32[288,128]{0,1:T(8,128)}, u32[]{:S(2)}, u32[]{:S(2)}) collective-permute-start(f32[288,128]{0,1:T(8,128)} %copy.318), channel_id=1, source_target_pairs={{1,0},{2,1},{3,2},{4,3},{5,4},{6,5},{7,6},{8,7},{9,8},{10,9},{11,1... | collective-permute-start | bytes 442376 | tf_op jit(solution)/shard_map/ppermute | solution.py:18
  416.9 14.8 %gather_fusion.13 = f32[6912,128]{1,0:T(8,128)} fusion(f32[6912,128]{1,0:T(8,128)S(1)} %convolution_dynamic-update-slice_fusion.12, s32[7168]{0:T(1024)} %pad_clamp_fusion), kind=kCustom, calls=%fused_computation.13 | custom fusion | bytes 7105536 | tf_op jit(solution)/shard_map/gather | solution.py:158
  446.7 6.7 %fusion.29 = f32[6912,25]{1,0:T(8,128)} fusion(f32[6912,128]{1,0:T(8,128)} %gather_fusion.13, f32[6912,128]{1,0:T(8,128)S(1)} %fusion.2, f32[6912,128]{1,0:T(8,128)S(1)} %convolution_dynamic-update-slice_fusion.12, f32[6,25]{1,0:T(8,128)S(1)} %copy-done.98, pred[6912]{0:T(1024)(128)(4,1)S(1)} %broadcast_compare_fusion), kind=kLoop, calls=%fused_computation.60 | loop fusion | flops 1209600 | bytes 4154712 | tf_op jit(solution)/shard_map/sub | solution.py:161
  472.3 7.9 %collective-permute-start.15 = (f32[288,128]{0,1:T(8,128)}, f32[288,128]{0,1:T(8,128)}, u32[]{:S(2)}, u32[]{:S(2)}) collective-permute-start(f32[288,128]{0,1:T(8,128)} %copy.320), channel_id=1, source_target_pairs={{1,0},{2,1},{3,2},{4,3},{5,4},{6,5},{7,6},{8,7},{9,8},{10,9},{11,1... | collective-permute-start | bytes 442376 | tf_op jit(solution)/shard_map/ppermute | solution.py:18
  482.0 14.8 %gather_fusion.15 = f32[6912,128]{1,0:T(8,128)} fusion(f32[6912,128]{1,0:T(8,128)S(1)} %convolution_dynamic-update-slice_fusion.6, s32[7168]{0:T(1024)} %pad_clamp_fusion), kind=kCustom, calls=%fused_computation.15 | custom fusion | bytes 7105536 | tf_op jit(solution)/shard_map/gather | solution.py:158
  505.9 7.8 %fusion.1 = f32[6912,128]{1,0:T(8,128)} fusion(bf16[576,128]{1,0:T(8,128)(2,1)} %concatenate.184, s32[576]{0:T(1024)} %pad_add_fusion), kind=kOutput, calls=%fused_computation.28 | convolution fusion | flops 1023197184 | bytes 3688704 | tf_op jit(solution)/shard_map/dot_general | solution.py:143
  513.7 9.8 %fusion.30 = f32[6912,25]{1,0:T(8,128)} fusion(f32[6912,128]{1,0:T(8,128)} %gather_fusion.15, f32[6912,128]{1,0:T(8,128)} %fusion.1, f32[6912,128]{1,0:T(8,128)S(1)} %convolution_dynamic-update-slice_fusion.6, f32[6,25]{1,0:T(8,128)S(1)} %copy-done.98, pred[6912]{0:T(1024)(128)(4,1)S(1)} %broadcast_compare_fusion), kind=kLoop, calls=%fused_computation.61 | loop fusion | flops 1209600 | bytes 4154712 | tf_op jit(solution)/shard_map/sub | solution.py:161
  545.5 8.0 %collective-permute-start.17 = (f32[288,128]{0,1:T(8,128)}, f32[288,128]{0,1:T(8,128)}, u32[]{:S(2)}, u32[]{:S(2)}) collective-permute-start(f32[288,128]{0,1:T(8,128)} %copy.322), channel_id=1, source_target_pairs={{1,0},{2,1},{3,2},{4,3},{5,4},{6,5},{7,6},{8,7},{9,8},{10,9},{11,1... | collective-permute-start | bytes 442376 | tf_op jit(solution)/shard_map/ppermute | solution.py:18
  555.4 14.8 %gather_fusion.17 = f32[6912,128]{1,0:T(8,128)} fusion(f32[6912,128]{1,0:T(8,128)S(1)} %convolution_dynamic-update-slice_fusion, s32[7168]{0:T(1024)} %pad_clamp_fusion), kind=kCustom, calls=%fused_computation.17 | custom fusion | bytes 7105536 | tf_op jit(solution)/shard_map/gather | solution.py:158
  587.3 6.8 %fusion.31 = f32[6912,25]{1,0:T(8,128)} fusion(f32[6912,128]{1,0:T(8,128)} %gather_fusion.17, f32[6912,128]{1,0:T(8,128)S(1)} %fusion, f32[6912,128]{1,0:T(8,128)S(1)} %convolution_dynamic-update-slice_fusion, f32[6,25]{1,0:T(8,128)S(1)} %copy-done.98, pred[6912]{0:T(1024)(128)(4,1)S(1)} %broadcast_compare_fusion), kind=kLoop, calls=%fused_computation.62 | loop fusion | flops 1209600 | bytes 4154712 | tf_op jit(solution)/shard_map/sub | solution.py:161
  (548 shorter events, 326.2 us)
Async XLA Ops:
  18.1 30.0 %collective-permute-start.1 = (f32[288,128]{0,1:T(8,128)}, f32[288,128]{0,1:T(8,128)}, u32[]{:S(2)}, u32[]{:S(2)}) collective-permute-start(f32[288,128]{0,1:T(8,128)} %copy.306), channel_id=1, source_target_pairs={{1,0},{2,1},{3,2},{4,3},{5,4},{6,5},{7,6},{8,7},{9,8},{10,9},{11,1... | collective-permute-start | bytes 442376 | tf_op jit(solution)/shard_map/ppermute | solution.py:18
  27.6 20.5 %collective-permute-start = (f32[288,128]{0,1:T(8,128)}, f32[288,128]{0,1:T(8,128)}, u32[]{:S(2)}, u32[]{:S(2)}) collective-permute-start(f32[288,128]{0,1:T(8,128)} %copy.305), channel_id=1, source_target_pairs={{0,1},{1,2},{2,3},{3,4},{4,5},{5,6},{6,7},{7,8},{8,9},{9,10},{10,1... | collective-permute-start | bytes 442376 | tf_op jit(solution)/shard_map/ppermute | solution.py:18
  31.6 15.1 %copy-start.128 = (s32[288]{0:T(512)S(1)}, s32[288]{0:T(512)}, u32[]{:S(2)}) copy-start(s32[288]{0:T(512)} %param.30) | copy-start | bytes 3460
  89.9 25.9 %collective-permute-start.3 = (f32[288,128]{0,1:T(8,128)}, f32[288,128]{0,1:T(8,128)}, u32[]{:S(2)}, u32[]{:S(2)}) collective-permute-start(f32[288,128]{0,1:T(8,128)} %copy.308), channel_id=1, source_target_pairs={{1,0},{2,1},{3,2},{4,3},{5,4},{6,5},{7,6},{8,7},{9,8},{10,9},{11,1... | collective-permute-start | bytes 442376 | tf_op jit(solution)/shard_map/ppermute | solution.py:18
  97.8 18.0 %collective-permute-start.2 = (f32[288,128]{0,1:T(8,128)}, f32[288,128]{0,1:T(8,128)}, u32[]{:S(2)}, u32[]{:S(2)}) collective-permute-start(f32[288,128]{0,1:T(8,128)} %copy.307), channel_id=1, source_target_pairs={{0,1},{1,2},{2,3},{3,4},{4,5},{5,6},{6,7},{7,8},{8,9},{9,10},{10,1... | collective-permute-start | bytes 442376 | tf_op jit(solution)/shard_map/ppermute | solution.py:18
  155.9 25.9 %collective-permute-start.5 = (f32[288,128]{0,1:T(8,128)}, f32[288,128]{0,1:T(8,128)}, u32[]{:S(2)}, u32[]{:S(2)}) collective-permute-start(f32[288,128]{0,1:T(8,128)} %copy.310), channel_id=1, source_target_pairs={{1,0},{2,1},{3,2},{4,3},{5,4},{6,5},{7,6},{8,7},{9,8},{10,9},{11,1... | collective-permute-start | bytes 442376 | tf_op jit(solution)/shard_map/ppermute | solution.py:18
  163.8 18.0 %collective-permute-start.4 = (f32[288,128]{0,1:T(8,128)}, f32[288,128]{0,1:T(8,128)}, u32[]{:S(2)}, u32[]{:S(2)}) collective-permute-start(f32[288,128]{0,1:T(8,128)} %copy.309), channel_id=1, source_target_pairs={{0,1},{1,2},{2,3},{3,4},{4,5},{5,6},{6,7},{7,8},{8,9},{9,10},{10,1... | collective-permute-start | bytes 442376 | tf_op jit(solution)/shard_map/ppermute | solution.py:18
  222.7 34.2 %all-to-all-start = ((f32[128,18,125]{2,1,0:T(8,128)}), f32[128,18,125]{2,1,0:T(8,128)S(1)}, u32[]{:S(2)}, u32[]{:S(2)}) async-start(f32[128,18,125]{2,1,0:T(8,128)} %all_to_all.16), calls=%async_computation | async-start | bytes 3145728 | tf_op jit(solution)/shard_map/all_to_all | solution.py:250
  232.6 24.8 %copy-start.126 = (s32[2304]{0:T(1024)S(1)}, s32[2304]{0:T(1024)}, u32[]{:S(2)}) copy-start(s32[2304]{0:T(1024)} %param.27) | copy-start | bytes 27652
  261.2 7.7 %collective-permute-start.7 = (f32[64,128]{0,1:T(8,128)S(1)}, f32[64,128]{0,1:T(8,128)S(1)}, u32[]{:S(2)}, u32[]{:S(2)}) collective-permute-start(f32[64,128]{0,1:T(8,128)S(1)} %copy.312), channel_id=1, source_target_pairs={{1,0},{2,1},{3,2},{4,3},{5,4},{6,5},{7,6},{8,7},{9,8},{10,9},{11,1... | collective-permute-start | bytes 98312 | tf_op jit(solution)/shard_map/ppermute | solution.py:18
  264.1 9.8 %collective-permute-start.6 = (f32[64,128]{0,1:T(8,128)S(1)}, f32[64,128]{0,1:T(8,128)S(1)}, u32[]{:S(2)}, u32[]{:S(2)}) collective-permute-start(f32[64,128]{0,1:T(8,128)S(1)} %copy.311), channel_id=1, source_target_pairs={{0,1},{1,2},{2,3},{3,4},{4,5},{5,6},{6,7},{7,8},{8,9},{9,10},{10,1... | collective-permute-start | bytes 98312 | tf_op jit(solution)/shard_map/ppermute | solution.py:18
  279.2 7.4 %collective-permute-start.9 = (f32[64,128]{0,1:T(8,128)S(1)}, f32[64,128]{0,1:T(8,128)S(1)}, u32[]{:S(2)}, u32[]{:S(2)}) collective-permute-start(f32[64,128]{0,1:T(8,128)S(1)} %copy.314), channel_id=1, source_target_pairs={{1,0},{2,1},{3,2},{4,3},{5,4},{6,5},{7,6},{8,7},{9,8},{10,9},{11,1... | collective-permute-start | bytes 98312 | tf_op jit(solution)/shard_map/ppermute | solution.py:18
  282.0 9.8 %collective-permute-start.8 = (f32[64,128]{0,1:T(8,128)S(1)}, f32[64,128]{0,1:T(8,128)S(1)}, u32[]{:S(2)}, u32[]{:S(2)}) collective-permute-start(f32[64,128]{0,1:T(8,128)S(1)} %copy.313), channel_id=1, source_target_pairs={{0,1},{1,2},{2,3},{3,4},{4,5},{5,6},{6,7},{7,8},{8,9},{9,10},{10,1... | collective-permute-start | bytes 98312 | tf_op jit(solution)/shard_map/ppermute | solution.py:18
  346.4 20.1 %collective-permute-start.11 = (f32[288,128]{0,1:T(8,128)}, f32[288,128]{0,1:T(8,128)}, u32[]{:S(2)}, u32[]{:S(2)}) collective-permute-start(f32[288,128]{0,1:T(8,128)} %copy.316), channel_id=1, source_target_pairs={{1,0},{2,1},{3,2},{4,3},{5,4},{6,5},{7,6},{8,7},{9,8},{10,9},{11,1... | collective-permute-start | bytes 442376 | tf_op jit(solution)/shard_map/ppermute | solution.py:18
  349.3 17.2 %collective-permute-start.10 = (f32[288,128]{0,1:T(8,128)}, f32[288,128]{0,1:T(8,128)}, u32[]{:S(2)}, u32[]{:S(2)}) collective-permute-start(f32[288,128]{0,1:T(8,128)} %copy.315), channel_id=1, source_target_pairs={{0,1},{1,2},{2,3},{3,4},{4,5},{5,6},{6,7},{7,8},{8,9},{9,10},{10,1... | collective-permute-start | bytes 442376 | tf_op jit(solution)/shard_map/ppermute | solution.py:18
  407.1 24.6 %collective-permute-start.13 = (f32[288,128]{0,1:T(8,128)}, f32[288,128]{0,1:T(8,128)}, u32[]{:S(2)}, u32[]{:S(2)}) collective-permute-start(f32[288,128]{0,1:T(8,128)} %copy.318), channel_id=1, source_target_pairs={{1,0},{2,1},{3,2},{4,3},{5,4},{6,5},{7,6},{8,7},{9,8},{10,9},{11,1... | collective-permute-start | bytes 442376 | tf_op jit(solution)/shard_map/ppermute | solution.py:18
  414.9 16.7 %collective-permute-start.12 = (f32[288,128]{0,1:T(8,128)}, f32[288,128]{0,1:T(8,128)}, u32[]{:S(2)}, u32[]{:S(2)}) collective-permute-start(f32[288,128]{0,1:T(8,128)} %copy.317), channel_id=1, source_target_pairs={{0,1},{1,2},{2,3},{3,4},{4,5},{5,6},{6,7},{7,8},{8,9},{9,10},{10,1... | collective-permute-start | bytes 442376 | tf_op jit(solution)/shard_map/ppermute | solution.py:18
  472.3 24.6 %collective-permute-start.15 = (f32[288,128]{0,1:T(8,128)}, f32[288,128]{0,1:T(8,128)}, u32[]{:S(2)}, u32[]{:S(2)}) collective-permute-start(f32[288,128]{0,1:T(8,128)} %copy.320), channel_id=1, source_target_pairs={{1,0},{2,1},{3,2},{4,3},{5,4},{6,5},{7,6},{8,7},{9,8},{10,9},{11,1... | collective-permute-start | bytes 442376 | tf_op jit(solution)/shard_map/ppermute | solution.py:18
  480.1 16.7 %collective-permute-start.14 = (f32[288,128]{0,1:T(8,128)}, f32[288,128]{0,1:T(8,128)}, u32[]{:S(2)}, u32[]{:S(2)}) collective-permute-start(f32[288,128]{0,1:T(8,128)} %copy.319), channel_id=1, source_target_pairs={{0,1},{1,2},{2,3},{3,4},{4,5},{5,6},{6,7},{7,8},{8,9},{9,10},{10,1... | collective-permute-start | bytes 442376 | tf_op jit(solution)/shard_map/ppermute | solution.py:18
  505.9 23.7 %slice-start = ((s8[5308416]{0:T(1024)(128)(4,1)}), s8[4194304]{0:T(1024)(128)(4,1)S(1)}, s32[]{:S(2)}) async-start(s8[5308416]{0:T(1024)(128)(4,1)} %bitcast.301), calls=%async_computation.2 | async-start | bytes 8388608
  513.7 15.9 %slice-start.1 = ((s8[5308416]{0:T(1024)(128)(4,1)}), s8[1114112]{0:T(1024)(128)(4,1)S(1)}, s32[]{:S(2)}) async-start(s8[5308416]{0:T(1024)(128)(4,1)} %bitcast.301), calls=%async_computation.3 | async-start | bytes 2228224
  545.5 35.9 %copy-start.143 = (s32[576]{0:T(1024)S(1)}, s32[576]{0:T(1024)}, u32[]{:S(2)}) copy-start(s32[576]{0:T(1024)} %pad_add_fusion) | copy-start | bytes 6916
  545.5 26.8 %collective-permute-start.17 = (f32[288,128]{0,1:T(8,128)}, f32[288,128]{0,1:T(8,128)}, u32[]{:S(2)}, u32[]{:S(2)}) collective-permute-start(f32[288,128]{0,1:T(8,128)} %copy.322), channel_id=1, source_target_pairs={{1,0},{2,1},{3,2},{4,3},{5,4},{6,5},{7,6},{8,7},{9,8},{10,9},{11,1... | collective-permute-start | bytes 442376 | tf_op jit(solution)/shard_map/ppermute | solution.py:18
  553.4 18.8 %collective-permute-start.16 = (f32[288,128]{0,1:T(8,128)}, f32[288,128]{0,1:T(8,128)}, u32[]{:S(2)}, u32[]{:S(2)}) collective-permute-start(f32[288,128]{0,1:T(8,128)} %copy.321), channel_id=1, source_target_pairs={{0,1},{1,2},{2,3},{3,4},{4,5},{5,6},{6,7},{7,8},{8,9},{9,10},{10,1... | collective-permute-start | bytes 442376 | tf_op jit(solution)/shard_map/ppermute | solution.py:18
  (144 other events, 695.1 us)

commit v2 on v0

--- a/solution.py
+++ b/solution.py
@@ -125,15 +125,17 @@
 
 def level_plan(local_ids, left_ids, right_ids):
     face_count = local_ids.shape[0]
-    has_local = local_ids >= 0
-    source = jnp.where(has_local, local_ids, 0)
+    shared = left_ids.shape[0]
+    zero_row = face_count + 2 * shared
+    source = jnp.where(local_ids >= 0, local_ids, zero_row)
+    lanes = jnp.arange(shared, dtype=jnp.int32)
+    source = source.at[left_ids].set(face_count + lanes).at[right_ids].set(face_count + shared + lanes)
     send_ids = jnp.concatenate([left_ids, right_ids])
-    onehot = onehot_of(jnp.arange(face_count, dtype=jnp.int32), send_ids)
-    return has_local, source, send_ids, onehot
+    return source, send_ids
 
 
 def apply_level(vector_t, scale_col, plan, mats):
-    has_local, source, send_ids, onehot = plan
+    source, send_ids = plan
     stiffness_t, pick, fold, weight = mats
     elem_count = vector_t.shape[0]
     shared = send_ids.shape[0] // 2
@@ -143,9 +145,10 @@
     sent = faces[send_ids]
     from_left = passed_along(sent[shared:], AXES, 1)
     from_right = passed_along(sent[:shared], AXES, -1)
-    partner = jnp.where(has_local[:, None], faces[source], 0.0)
-    received = jnp.concatenate([from_left, from_right], axis=0)
-    partner = partner + place(onehot, received)
+    extended = jnp.concatenate(
+        [faces, from_left, from_right, jnp.zeros((8, faces.shape[1]), faces.dtype)], axis=0
+    )
+    partner = extended[source]
     jump = (faces - partner).reshape(6, elem_count, 128) * weight[:, None, :]
     folded = lax.dot_general(
         jump, fold, (((2,), (1,)), ((0,), (0,))), precision=highest

time: 511 us -> 536 us (1.049); the launches traced: 508 us -> 527 us
  local copies, waits for them, and re-layouts: 163 us -> 187 us
  waiting for transfers between devices: 25.8 us -> 47.4 us
  other arithmetic: 58.8 us -> 46 us
  starting transfers between devices: 92.7 us -> 86 us
  matrix products: 130 us -> 124 us
    dot_general x13 -> x4, matrix products: 55.8 us -> 9.15 us  [place(): jnp.dot(onehot, jnp.concatenate(parts, axis=1), preferred_element_type=jn...]
    dot_general x54, matrix products: 32.4 us -> 74.8 us  [apply_level(): jnp.dot(vector_t, pick[f], precision=highest)]
    ppermute x18, waiting for transfers between devices: 1.43 us -> 26.9 us  [passed_along(): return lax.ppermute(block, axis, route)]
    gather x9, local copies, waits for them, and re-layouts: 17.3 us -> 30.3 us  [apply_level(): sent = faces[send_ids]]
    slice x9, local copies, waits for them, and re-layouts: 12.1 us -> 1.92 us  [apply_level(): from_right = passed_along(sent[:shared], AXES, -1)]
    gather x9, local copies, waits for them, and re-layouts: 110 us -> 119 us  [apply_level(): partner = extended[source]]
    scatter x0 -> x4, local copies, waits for them, and re-layouts: none -> 7.75 us  [level_plan(): source.at[left_ids].set(face_count + lanes).at[right_ids]]
    transpose x1, other arithmetic: 15 us -> 7.37 us  [on_device(): return (final_x.T, final_r.T)]
  transfers between devices with their start and end apart: 19 -> 19, of which waited for: 2 -> 13; matrix products, arithmetic and copies ran while one was open for 25% -> 3% of each run, Pallas kernels for 0% -> 0%
where the time goes in v2:
time: 536 us; the launch traced here: 527 us
  local copies, waits for them, and re-layouts  187 us (35%)
  matrix products  124 us (23%)
  starting transfers between devices  86 us (16%)
  waiting for transfers between devices  47.4 us (9%)
  other arithmetic  46 us (9%)
  blocking collectives  33.4 us (6%)
    gather x9, local copies, waits for them, and re-layouts, apply_level(): partner = extended[source]  119 us
    ppermute x18, starting transfers between devices, passed_along(): return lax.ppermute(block, axis, route)  81.1 us
    dot_general x54, matrix products, apply_level(): jnp.dot(vector_t, pick[f], precision=highest)  74.8 us
    all_to_all x1, blocking collectives, on_device(): returned = lax.all_to_all(filled, AXES, 0, 0, tiled=True)  33.4 us
    gather x9, local copies, waits for them, and re-layouts, apply_level(): sent = faces[send_ids]  30.3 us
    sub x9, other arithmetic, apply_level(): jump = (faces - partner).reshape(6, elem_count, 128) * weight[:, None, :]  27.1 us
    ppermute x18, waiting for transfers between devices, passed_along(): return lax.ppermute(block, axis, route)  26.9 us
    dot_general x9, matrix products, apply_level(): lax.dot_general(jump, fold, (((2,), (1,)), ((0,), (0,))), precision=highest)  22.2 us
  transfers between devices with their start and end apart: 19, of which 13 were waited for; matrix products, arithmetic and copies ran while one was open for 3% of the time, Pallas kernels for 0%

profile of v2, /device:TPU:2, one launch (start us, length us, event | category | flops | bytes accessed | tf_op | source)
XLA Modules:
  0.0 527.3 jit_solution(4747003636947399046)
XLA Ops:
  20.1 7.8 %collective-permute-start.1 = (f32[288,128]{1,0:T(8,128)S(1)}, f32[288,128]{1,0:T(8,128)S(1)}, u32[]{:S(2)}, u32[]{:S(2)}) collective-permute-start(f32[288,128]{1,0:T(8,128)S(1)} %get-tuple-element.128), channel_id=1, source_target_pairs={{1,0},{2,1},{3,2},{4,3},{5,4},{6,5},{7,6},{8,7},{9,8},{10,9},{11,1... | collective-permute-start | bytes 442376 | tf_op jit(solution)/shard_map/ppermute | solution.py:18
  40.5 15.6 %gather_fusion.1 = f32[6912,128]{1,0:T(8,128)} fusion(f32[7496,128]{1,0:T(8,128)} %constant_dynamic-update-slice_fusion.6, s32[7168]{0:T(1024)S(1)} %pad_clamp_fusion), kind=kCustom, calls=%fused_computation.1 | custom fusion | bytes 7105536 | tf_op jit(solution)/shard_map/gather | solution.py:151
  77.1 5.4 %collective-permute-start.3 = (f32[288,128]{1,0:T(8,128)S(1)}, f32[288,128]{1,0:T(8,128)S(1)}, u32[]{:S(2)}, u32[]{:S(2)}) collective-permute-start(f32[288,128]{1,0:T(8,128)S(1)} %get-tuple-element.126), channel_id=1, source_target_pairs={{1,0},{2,1},{3,2},{4,3},{5,4},{6,5},{7,6},{8,7},{9,8},{10,9},{11,1... | collective-permute-start | bytes 442376 | tf_op jit(solution)/shard_map/ppermute | solution.py:18
  85.3 7.9 %collective-permute-done.2 = f32[288,128]{1,0:T(8,128)S(1)} collective-permute-done((f32[288,128]{1,0:T(8,128)S(1)}, f32[288,128]{1,0:T(8,128)S(1)}, u32[]{:S(2)}, u32[]{:S(2)}) %collective-permute-start.2) | collective-permute-done | bytes 147488 | tf_op jit(solution)/shard_map/ppermute | solution.py:18
  95.1 15.6 %gather_fusion.3 = f32[6912,128]{1,0:T(8,128)} fusion(f32[7496,128]{1,0:T(8,128)} %constant_dynamic-update-slice_fusion.21, s32[7168]{0:T(1024)S(1)} %pad_clamp_fusion), kind=kCustom, calls=%fused_computation.3 | custom fusion | bytes 7105536 | tf_op jit(solution)/shard_map/gather | solution.py:151
  128.0 4.2 gather_fusion.4
  139.3 6.5 %collective-permute-done.4 = f32[288,128]{1,0:T(8,128)S(1)} collective-permute-done((f32[288,128]{1,0:T(8,128)S(1)}, f32[288,128]{1,0:T(8,128)S(1)}, u32[]{:S(2)}, u32[]{:S(2)}) %collective-permute-start.4) | collective-permute-done | bytes 147488 | tf_op jit(solution)/shard_map/ppermute | solution.py:18
  147.8 16.9 %gather_fusion.5 = f32[6912,128]{1,0:T(8,128)} fusion(f32[7496,128]{1,0:T(8,128)} %constant_dynamic-update-slice_fusion.36, s32[7168]{0:T(1024)} %copy-done.50), kind=kCustom, calls=%fused_computation.5 | custom fusion | bytes 7105536 | tf_op jit(solution)/shard_map/gather | solution.py:151
  172.7 4.5 fusion.269
  184.7 4.9 all-to-all-start
  193.2 20.5 %all-to-all-done = f32[128,18,125]{2,1,0:T(8,128)} async-done(((f32[128,18,125]{2,1,0:T(8,128)}), f32[128,18,125]{2,1,0:T(8,128)}, u32[]{:S(2)}, u32[]{:S(2)}) %all-to-all-start) | async-done | bytes 1152032 | tf_op jit(solution)/shard_map/all_to_all | solution.py:240
  224.4 7.9 %collective-permute-start.7 = (f32[64,128]{1,0:T(8,128)S(1)}, f32[64,128]{1,0:T(8,128)S(1)}, u32[]{:S(2)}, u32[]{:S(2)}) collective-permute-start(f32[64,128]{1,0:T(8,128)S(1)} %get-tuple-element.159), channel_id=1, source_target_pairs={{1,0},{2,1},{3,2},{4,3},{5,4},{6,5},{7,6},{8,7},{9,8},{10,9},{11,1... | collective-permute-start | bytes 98312 | tf_op jit(solution)/shard_map/ppermute | solution.py:18
  248.6 7.9 %collective-permute-start.9 = (f32[64,128]{1,0:T(8,128)S(1)}, f32[64,128]{1,0:T(8,128)S(1)}, u32[]{:S(2)}, u32[]{:S(2)}) collective-permute-start(f32[64,128]{1,0:T(8,128)S(1)} %get-tuple-element.157), channel_id=1, source_target_pairs={{1,0},{2,1},{3,2},{4,3},{5,4},{6,5},{7,6},{8,7},{9,8},{10,9},{11,1... | collective-permute-start | bytes 98312 | tf_op jit(solution)/shard_map/ppermute | solution.py:18
  267.1 33.4 %all_to_all.24 = f32[128,18,125]{2,1,0:T(8,128)} all-to-all(f32[128,18,125]{2,1,0:T(8,128)} %all_to_all.19), channel_id=1, replica_groups=mesh['elem'=16,'sub'=8] {'elem','sub'}, dimensions={0} | all-to-all | bytes 2304000 | tf_op jit(solution)/shard_map/all_to_all | solution.py:246
  307.0 4.6 fusion.115
  329.7 7.9 %collective-permute-start.11 = (f32[288,128]{1,0:T(8,128)S(1)}, f32[288,128]{1,0:T(8,128)S(1)}, u32[]{:S(2)}, u32[]{:S(2)}) collective-permute-start(f32[288,128]{1,0:T(8,128)S(1)} %get-tuple-element.122), channel_id=1, source_target_pairs={{1,0},{2,1},{3,2},{4,3},{5,4},{6,5},{7,6},{8,7},{9,8},{10,9},{11,1... | collective-permute-start | bytes 442376 | tf_op jit(solution)/shard_map/ppermute | solution.py:18
  341.5 15.6 %gather_fusion.11 = f32[6912,128]{1,0:T(8,128)} fusion(f32[7496,128]{1,0:T(8,128)} %constant_dynamic-update-slice_fusion.81, s32[7168]{0:T(1024)S(1)} %copy-done.51), kind=kCustom, calls=%fused_computation.11 | custom fusion | bytes 7105536 | tf_op jit(solution)/shard_map/gather | solution.py:151
  381.1 8.0 %collective-permute-start.13 = (f32[288,128]{1,0:T(8,128)S(1)}, f32[288,128]{1,0:T(8,128)S(1)}, u32[]{:S(2)}, u32[]{:S(2)}) collective-permute-start(f32[288,128]{1,0:T(8,128)S(1)} %get-tuple-element.120), channel_id=1, source_target_pairs={{1,0},{2,1},{3,2},{4,3},{5,4},{6,5},{7,6},{8,7},{9,8},{10,9},{11,1... | collective-permute-start | bytes 442376 | tf_op jit(solution)/shard_map/ppermute | solution.py:18
  393.1 15.8 %gather_fusion.13 = f32[6912,128]{1,0:T(8,128)} fusion(f32[7496,128]{1,0:T(8,128)} %constant_dynamic-update-slice_fusion.96, s32[7168]{0:T(1024)S(1)} %copy-done.51), kind=kCustom, calls=%fused_computation.13 | custom fusion | bytes 7105536 | tf_op jit(solution)/shard_map/gather | solution.py:151
  432.8 8.0 %collective-permute-start.15 = (f32[288,128]{1,0:T(8,128)S(1)}, f32[288,128]{1,0:T(8,128)S(1)}, u32[]{:S(2)}, u32[]{:S(2)}) collective-permute-start(f32[288,128]{1,0:T(8,128)S(1)} %get-tuple-element.118), channel_id=1, source_target_pairs={{1,0},{2,1},{3,2},{4,3},{5,4},{6,5},{7,6},{8,7},{9,8},{10,9},{11,1... | collective-permute-start | bytes 442376 | tf_op jit(solution)/shard_map/ppermute | solution.py:18
  444.7 15.8 %gather_fusion.15 = f32[6912,128]{1,0:T(8,128)} fusion(f32[7496,128]{1,0:T(8,128)} %constant_dynamic-update-slice_fusion.111, s32[7168]{0:T(1024)S(1)} %copy-done.52), kind=kCustom, calls=%fused_computation.15 | custom fusion | bytes 7105536 | tf_op jit(solution)/shard_map/gather | solution.py:151
  467.8 7.4 %add_bitcast_fusion = (f32[125,1152]{0,1:T(8,128)}, f32[1152,125]{1,0:T(8,128)S(1)}) fusion(f32[1152,125]{1,0:T(8,128)S(1)} %get-tuple-element.8, f32[1152,125]{1,0:T(8,128)S(1)} %get-tuple-element.172, f32[1152,125]{1,0:T(8,128)S(1)} %get-tuple-element.170, f32[125,1152]{0,1:T(8,128)S(1)} %copy.42, f32[125]{0:T(128)S(1)} %copy-done.106, ...), kind=kLoop, calls=%fused_computation.179 | loop fusion | flops 3888000 | bytes 10383976 | tf_op jit(solution)/shard_map/transpose | solution.py:251
  490.8 8.0 %collective-permute-start.17 = (f32[288,128]{1,0:T(8,128)S(1)}, f32[288,128]{1,0:T(8,128)S(1)}, u32[]{:S(2)}, u32[]{:S(2)}) collective-permute-start(f32[288,128]{1,0:T(8,128)S(1)} %get-tuple-element.116), channel_id=1, source_target_pairs={{1,0},{2,1},{3,2},{4,3},{5,4},{6,5},{7,6},{8,7},{9,8},{10,9},{11,1... | collective-permute-start | bytes 442376 | tf_op jit(solution)/shard_map/ppermute | solution.py:18
  502.8 15.8 %gather_fusion.17 = f32[6912,128]{1,0:T(8,128)} fusion(f32[7496,128]{1,0:T(8,128)} %constant_dynamic-update-slice_fusion.126, s32[7168]{0:T(1024)S(1)} %copy-done.53), kind=kCustom, calls=%fused_computation.17 | custom fusion | bytes 7105536 | tf_op jit(solution)/shard_map/gather | solution.py:151
  (427 shorter events, 258.4 us)
Async XLA Ops:
  20.1 19.2 %collective-permute-start.1 = (f32[288,128]{1,0:T(8,128)S(1)}, f32[288,128]{1,0:T(8,128)S(1)}, u32[]{:S(2)}, u32[]{:S(2)}) collective-permute-start(f32[288,128]{1,0:T(8,128)S(1)} %get-tuple-element.128), channel_id=1, source_target_pairs={{1,0},{2,1},{3,2},{4,3},{5,4},{6,5},{7,6},{8,7},{9,8},{10,9},{11,1... | collective-permute-start | bytes 442376 | tf_op jit(solution)/shard_map/ppermute | solution.py:18
  27.9 10.7 %collective-permute-start = (f32[288,128]{1,0:T(8,128)S(1)}, f32[288,128]{1,0:T(8,128)S(1)}, u32[]{:S(2)}, u32[]{:S(2)}) collective-permute-start(f32[288,128]{1,0:T(8,128)S(1)} %get-tuple-element.129), channel_id=1, source_target_pairs={{0,1},{1,2},{2,3},{3,4},{4,5},{5,6},{6,7},{7,8},{8,9},{9,10},{10,1... | collective-permute-start | bytes 442376 | tf_op jit(solution)/shard_map/ppermute | solution.py:18
  36.1 59.0 %copy-start.50 = (s32[7168]{0:T(1024)}, s32[7168]{0:T(1024)S(1)}, u32[]{:S(2)}) copy-start(s32[7168]{0:T(1024)S(1)} %pad_clamp_fusion) | copy-start | bytes 86020
  63.4 107.7 %copy-start.2 = (f32[1152,125]{1,0:T(8,128)}, f32[1152,125]{1,0:T(8,128)S(1)}, u32[]{:S(2)}) copy-start(f32[1152,125]{1,0:T(8,128)S(1)} %get-tuple-element.171) | copy-start | bytes 1728004
  77.1 16.8 %collective-permute-start.3 = (f32[288,128]{1,0:T(8,128)S(1)}, f32[288,128]{1,0:T(8,128)S(1)}, u32[]{:S(2)}, u32[]{:S(2)}) collective-permute-start(f32[288,128]{1,0:T(8,128)S(1)} %get-tuple-element.126), channel_id=1, source_target_pairs={{1,0},{2,1},{3,2},{4,3},{5,4},{6,5},{7,6},{8,7},{9,8},{10,9},{11,1... | collective-permute-start | bytes 442376 | tf_op jit(solution)/shard_map/ppermute | solution.py:18
  82.5 10.7 %collective-permute-start.2 = (f32[288,128]{1,0:T(8,128)S(1)}, f32[288,128]{1,0:T(8,128)S(1)}, u32[]{:S(2)}, u32[]{:S(2)}) collective-permute-start(f32[288,128]{1,0:T(8,128)S(1)} %get-tuple-element.127), channel_id=1, source_target_pairs={{0,1},{1,2},{2,3},{3,4},{4,5},{5,6},{6,7},{7,8},{8,9},{9,10},{10,1... | collective-permute-start | bytes 442376 | tf_op jit(solution)/shard_map/ppermute | solution.py:18
  118.0 53.1 %copy-start.4 = (f32[1152,125]{1,0:T(8,128)}, f32[1152,125]{1,0:T(8,128)S(1)}, u32[]{:S(2)}) copy-start(f32[1152,125]{1,0:T(8,128)S(1)} %get-tuple-element.173) | copy-start | bytes 1728004
  133.3 13.3 %collective-permute-start.5 = (f32[288,128]{1,0:T(8,128)S(1)}, f32[288,128]{1,0:T(8,128)S(1)}, u32[]{:S(2)}, u32[]{:S(2)}) collective-permute-start(f32[288,128]{1,0:T(8,128)S(1)} %get-tuple-element.124), channel_id=1, source_target_pairs={{1,0},{2,1},{3,2},{4,3},{5,4},{6,5},{7,6},{8,7},{9,8},{10,9},{11,1... | collective-permute-start | bytes 442376 | tf_op jit(solution)/shard_map/ppermute | solution.py:18
  135.2 10.7 %collective-permute-start.4 = (f32[288,128]{1,0:T(8,128)S(1)}, f32[288,128]{1,0:T(8,128)S(1)}, u32[]{:S(2)}, u32[]{:S(2)}) collective-permute-start(f32[288,128]{1,0:T(8,128)S(1)} %get-tuple-element.125), channel_id=1, source_target_pairs={{0,1},{1,2},{2,3},{3,4},{4,5},{5,6},{6,7},{7,8},{8,9},{9,10},{10,1... | collective-permute-start | bytes 442376 | tf_op jit(solution)/shard_map/ppermute | solution.py:18
  184.7 29.0 %all-to-all-start = ((f32[128,18,125]{2,1,0:T(8,128)}), f32[128,18,125]{2,1,0:T(8,128)}, u32[]{:S(2)}, u32[]{:S(2)}) async-start(f32[128,18,125]{2,1,0:T(8,128)} %all_to_all.16), calls=%async_computation | async-start | bytes 3145728 | tf_op jit(solution)/shard_map/all_to_all | solution.py:240
  222.4 9.8 %collective-permute-start.6 = (f32[64,128]{1,0:T(8,128)S(1)}, f32[64,128]{1,0:T(8,128)S(1)}, u32[]{:S(2)}, u32[]{:S(2)}) collective-permute-start(f32[64,128]{1,0:T(8,128)S(1)} %get-tuple-element.160), channel_id=1, source_target_pairs={{0,1},{1,2},{2,3},{3,4},{4,5},{5,6},{6,7},{7,8},{8,9},{9,10},{10,1... | collective-permute-start | bytes 98312 | tf_op jit(solution)/shard_map/ppermute | solution.py:18
  224.4 9.4 %collective-permute-start.7 = (f32[64,128]{1,0:T(8,128)S(1)}, f32[64,128]{1,0:T(8,128)S(1)}, u32[]{:S(2)}, u32[]{:S(2)}) collective-permute-start(f32[64,128]{1,0:T(8,128)S(1)} %get-tuple-element.159), channel_id=1, source_target_pairs={{1,0},{2,1},{3,2},{4,3},{5,4},{6,5},{7,6},{8,7},{9,8},{10,9},{11,1... | collective-permute-start | bytes 98312 | tf_op jit(solution)/shard_map/ppermute | solution.py:18
  246.7 9.8 %collective-permute-start.8 = (f32[64,128]{1,0:T(8,128)S(1)}, f32[64,128]{1,0:T(8,128)S(1)}, u32[]{:S(2)}, u32[]{:S(2)}) collective-permute-start(f32[64,128]{1,0:T(8,128)S(1)} %get-tuple-element.158), channel_id=1, source_target_pairs={{0,1},{1,2},{2,3},{3,4},{4,5},{5,6},{6,7},{7,8},{8,9},{9,10},{10,1... | collective-permute-start | bytes 98312 | tf_op jit(solution)/shard_map/ppermute | solution.py:18
  248.6 9.5 %collective-permute-start.9 = (f32[64,128]{1,0:T(8,128)S(1)}, f32[64,128]{1,0:T(8,128)S(1)}, u32[]{:S(2)}, u32[]{:S(2)}) collective-permute-start(f32[64,128]{1,0:T(8,128)S(1)} %get-tuple-element.157), channel_id=1, source_target_pairs={{1,0},{2,1},{3,2},{4,3},{5,4},{6,5},{7,6},{8,7},{9,8},{10,9},{11,1... | collective-permute-start | bytes 98312 | tf_op jit(solution)/shard_map/ppermute | solution.py:18
  320.9 20.7 %copy-start.51 = (s32[7168]{0:T(1024)S(1)}, s32[7168]{0:T(1024)}, u32[]{:S(2)}) copy-start(s32[7168]{0:T(1024)} %copy-done.50) | copy-start | bytes 86020
  327.8 10.7 %collective-permute-start.10 = (f32[288,128]{1,0:T(8,128)S(1)}, f32[288,128]{1,0:T(8,128)S(1)}, u32[]{:S(2)}, u32[]{:S(2)}) collective-permute-start(f32[288,128]{1,0:T(8,128)S(1)} %get-tuple-element.123), channel_id=1, source_target_pairs={{0,1},{1,2},{2,3},{3,4},{4,5},{5,6},{6,7},{7,8},{8,9},{9,10},{10,1... | collective-permute-start | bytes 442376 | tf_op jit(solution)/shard_map/ppermute | solution.py:18
  329.7 10.5 %collective-permute-start.11 = (f32[288,128]{1,0:T(8,128)S(1)}, f32[288,128]{1,0:T(8,128)S(1)}, u32[]{:S(2)}, u32[]{:S(2)}) collective-permute-start(f32[288,128]{1,0:T(8,128)S(1)} %get-tuple-element.122), channel_id=1, source_target_pairs={{1,0},{2,1},{3,2},{4,3},{5,4},{6,5},{7,6},{8,7},{9,8},{10,9},{11,1... | collective-permute-start | bytes 442376 | tf_op jit(solution)/shard_map/ppermute | solution.py:18
  379.2 10.8 %collective-permute-start.12 = (f32[288,128]{1,0:T(8,128)S(1)}, f32[288,128]{1,0:T(8,128)S(1)}, u32[]{:S(2)}, u32[]{:S(2)}) collective-permute-start(f32[288,128]{1,0:T(8,128)S(1)} %get-tuple-element.121), channel_id=1, source_target_pairs={{0,1},{1,2},{2,3},{3,4},{4,5},{5,6},{6,7},{7,8},{8,9},{9,10},{10,1... | collective-permute-start | bytes 442376 | tf_op jit(solution)/shard_map/ppermute | solution.py:18
  381.1 10.7 %collective-permute-start.13 = (f32[288,128]{1,0:T(8,128)S(1)}, f32[288,128]{1,0:T(8,128)S(1)}, u32[]{:S(2)}, u32[]{:S(2)}) collective-permute-start(f32[288,128]{1,0:T(8,128)S(1)} %get-tuple-element.120), channel_id=1, source_target_pairs={{1,0},{2,1},{3,2},{4,3},{5,4},{6,5},{7,6},{8,7},{9,8},{10,9},{11,1... | collective-permute-start | bytes 442376 | tf_op jit(solution)/shard_map/ppermute | solution.py:18
  423.9 20.8 %copy-start.52 = (s32[7168]{0:T(1024)S(1)}, s32[7168]{0:T(1024)}, u32[]{:S(2)}) copy-start(s32[7168]{0:T(1024)} %copy-done.50) | copy-start | bytes 86020
  430.8 10.8 %collective-permute-start.14 = (f32[288,128]{1,0:T(8,128)S(1)}, f32[288,128]{1,0:T(8,128)S(1)}, u32[]{:S(2)}, u32[]{:S(2)}) collective-permute-start(f32[288,128]{1,0:T(8,128)S(1)} %get-tuple-element.119), channel_id=1, source_target_pairs={{0,1},{1,2},{2,3},{3,4},{4,5},{5,6},{6,7},{7,8},{8,9},{9,10},{10,1... | collective-permute-start | bytes 442376 | tf_op jit(solution)/shard_map/ppermute | solution.py:18
  432.8 10.7 %collective-permute-start.15 = (f32[288,128]{1,0:T(8,128)S(1)}, f32[288,128]{1,0:T(8,128)S(1)}, u32[]{:S(2)}, u32[]{:S(2)}) collective-permute-start(f32[288,128]{1,0:T(8,128)S(1)} %get-tuple-element.118), channel_id=1, source_target_pairs={{1,0},{2,1},{3,2},{4,3},{5,4},{6,5},{7,6},{8,7},{9,8},{10,9},{11,1... | collective-permute-start | bytes 442376 | tf_op jit(solution)/shard_map/ppermute | solution.py:18
  488.9 11.0 %collective-permute-start.16 = (f32[288,128]{1,0:T(8,128)S(1)}, f32[288,128]{1,0:T(8,128)S(1)}, u32[]{:S(2)}, u32[]{:S(2)}) collective-permute-start(f32[288,128]{1,0:T(8,128)S(1)} %get-tuple-element.117), channel_id=1, source_target_pairs={{0,1},{1,2},{2,3},{3,4},{4,5},{5,6},{6,7},{7,8},{8,9},{9,10},{10,1... | collective-permute-start | bytes 442376 | tf_op jit(solution)/shard_map/ppermute | solution.py:18
  490.8 10.7 %collective-permute-start.17 = (f32[288,128]{1,0:T(8,128)S(1)}, f32[288,128]{1,0:T(8,128)S(1)}, u32[]{:S(2)}, u32[]{:S(2)}) collective-permute-start(f32[288,128]{1,0:T(8,128)S(1)} %get-tuple-element.116), channel_id=1, source_target_pairs={{1,0},{2,1},{3,2},{4,3},{5,4},{6,5},{7,6},{8,7},{9,8},{10,9},{11,1... | collective-permute-start | bytes 442376 | tf_op jit(solution)/shard_map/ppermute | solution.py:18
  (110 other events, 499.4 us)
